TPU v7x, 32 devices: a whole 2x2x4 slice. The times are simulated.
32 devices in a mesh: groups: 2 (over y), dp: 4 (over z), tensor: 4 (over x, core).
Axes of the slice: x: 2, y: 2, z: 4, core: 2. Of those that a mesh axis runs over, the one named last changes fastest.
Arguments:
- inputs: bfloat16 [2048, 8192], P(('groups', 'dp'), 'tensor'), parts along dimension 0, may hold values from -6 to 6
- cotangent: bfloat16 [2048, 8192], P(('groups', 'dp'), 'tensor'), parts along dimension 0, may hold values from -6 to 6
- up_blocks: bfloat16 [256, 64, 3, 256], P('dp', 'tensor'), may hold values from -0.21875 to 0.21875
- down_blocks: bfloat16 [256, 64, 3, 256], P('dp', 'tensor'), may hold values from -0.15625 to 0.15625
- low_left: bfloat16 [128, 8192], P(None, 'tensor'), may hold values from -0.0625 to 0.0625
- low_right: bfloat16 [128, 16384], P(None, 'tensor'), may hold values from -0.5 to 0.5
- up_pattern: int32 [64, 3], P('tensor'), may hold values from 0 to 7
- down_pattern: int32 [64, 3], P('tensor'), may hold values from 0 to 7
Outputs:
- grad_input: bfloat16 [2048, 8192], P(('groups', 'dp'), 'tensor'), parts along dimension 0
- grad_up: float32 [512, 64, 3, 256], P(('groups', 'dp'), 'tensor'), parts along dimension 0
- grad_down: float32 [512, 64, 3, 256], P(('groups', 'dp'), 'tensor'), parts along dimension 0
- grad_left: float32 [256, 8192], P(('groups', 'dp'), 'tensor'), parts along dimension 0
- grad_right: float32 [256, 16384], P(('groups', 'dp'), 'tensor'), parts along dimension 0
There are 2 independent parts, one for each index of `groups`. A program takes and returns all parts, laid end to end along the dimension named above; an argument that names none is the same for every part. Nothing has to cross between parts.
Inputs may be any that keep to these rules, and one draw needn't show every extreme that they name: `up_pattern`: feature block within a slice of 8 blocks. `down_pattern`: feature block within a slice of 8 blocks.
All inputs are finite; a program needn't handle non-finite values.
Results may differ from a plain program's by a relative error of at most 0.02.
Values may be sent and summed in bfloat16 or wider, within the bound.
No kernel may reach another device: no remote copies, remote signals or barrier semaphores. Data moves between devices by JAX's collectives and lax.ppermute only.
A program may use at most 128 MiB of HBM per device.

v0:
```python
import math

import jax
import jax.numpy as jnp
from jax import lax
from jax.sharding import PartitionSpec as P

root_coef = 0.7978845608028654
cubic_coef = 0.044715


def swapped(block, axis, distance):
    count = lax.axis_size(axis)
    route = []
    for low in range(count):
        high = low | 1 << distance
        if high != low and high < count:
            route += [(low, high), (high, low)]
    return lax.ppermute(block, axis, route)


def fetch_share(block):
    group_count = lax.axis_size("groups")
    rows = block.shape[0]
    if group_count == 1 or rows % group_count:
        return lax.all_gather(block, "dp", axis=0, tiled=True)
    share = rows // group_count
    mine = lax.dynamic_slice_in_dim(block, lax.axis_index("groups") * share, share, axis=0)
    return lax.all_gather(mine, "dp", axis=0, tiled=False)


def rotated(values, start):
    count = values.shape[0]
    doubled = jnp.concatenate([values, values], axis=0)
    return lax.dynamic_slice_in_dim(doubled, start % count, count, axis=0)


def swap_shares(fetched, block):
    group_count = lax.axis_size("groups")
    if group_count == 1 or block.shape[0] % group_count:
        return fetched
    group = lax.axis_index("groups")
    if group_count == 2:
        count = fetched.shape[0]
        me = lax.axis_index("dp")
        send = rotated(fetched, me + 1)[: count - 1]
        got = lax.ppermute(send, "groups", [(0, 1), (1, 0)])
        share = block.shape[0] // 2
        local = lax.dynamic_slice_in_dim(block, (1 - group) * share, share, axis=0)
        other = rotated(jnp.concatenate([got, local[None]], axis=0), count - 1 - me)
        received = [fetched, other]
    else:
        received = [fetched] + [
            lax.ppermute(
                fetched, "groups", [(g, (g + shift) % group_count) for g in range(group_count)]
            )
            for shift in range(1, group_count)
        ]
    reverse = jnp.stack(received[::-1], axis=1)
    doubled = jnp.concatenate([reverse, reverse], axis=1)
    ordered = lax.dynamic_slice_in_dim(doubled, group_count - 1 - group, group_count, axis=1)
    return ordered.reshape((-1,) + block.shape[1:])


def split_rows(values, axis, count):
    rows = values.shape[axis] // count
    return [lax.slice_in_dim(values, d * rows, (d + 1) * rows, axis=axis) for d in range(count)]


def butterfly_sum(values, axis):
    count = lax.axis_size(axis)
    if count & (count - 1):
        return lax.psum(values.astype(jnp.bfloat16), axis).astype(jnp.float32)
    total = values
    distance = 0
    while (1 << distance) < count:
        total = total + swapped(total, axis, distance)
        distance += 1
    return total


def gelu_pair(values):
    inner_arg = root_coef * (values + cubic_coef * values * values * values)
    tangent = jnp.tanh(inner_arg)
    forward = 0.5 * values * (1.0 + tangent)
    slopes = 0.5 * (1.0 + tangent) + 0.5 * values * (1.0 - tangent * tangent) * root_coef * (
        1.0 + 3.0 * cubic_coef * values * values
    )
    return (forward, slopes)


def pick_blocks(slices, pattern, block_size):
    picked = []
    for which_section, source in enumerate(slices):
        shaped = source.reshape(source.shape[0], -1, block_size)
        picked.append(jnp.take(shaped, pattern[:, which_section], axis=1))
    return jnp.stack(picked, axis=2)


def shards(
    inputs, cotangent, up_blocks, down_blocks, low_left, low_right, up_pattern, down_pattern
):
    tokens_here, width_here = inputs.shape
    block_size = up_blocks.shape[3]
    hidden_here = up_blocks.shape[1]
    section_count = up_blocks.shape[2]
    blocks_here = width_here // block_size
    dp_size = lax.axis_size("dp")
    inv_root = 1.0 / math.sqrt(tokens_here * dp_size)
    up_fetched = fetch_share(up_blocks)
    down_fetched = fetch_share(down_blocks)
    up_full = swap_shares(up_fetched, up_blocks)
    sources = [inputs] + [
        swapped(inputs, "tensor", level_bit) for level_bit in range(section_count - 1)
    ]
    selected = pick_blocks(sources, up_pattern, block_size)
    sparse = jnp.einsum("thsi,ihsj->thj", selected, up_full, preferred_element_type=jnp.float32)
    low_part = lax.dot_general(
        inputs, low_left, (((1,), (1,)), ((), ())), preferred_element_type=jnp.float32
    )
    low_sum = butterfly_sum(low_part, "tensor").astype(jnp.bfloat16)
    preact = sparse.reshape(tokens_here, -1) + jnp.dot(
        low_sum, low_right, preferred_element_type=jnp.float32
    )
    activated, slopes = gelu_pair(preact)
    hidden = activated.astype(jnp.bfloat16)
    picked = pick_blocks([cotangent] * section_count, down_pattern, block_size)
    hidden_blocks = hidden.reshape(tokens_here, hidden_here, block_size)
    down_parts = (
        jnp.stack(
            [
                jnp.einsum("thj,thso->hjso", rows, picked, preferred_element_type=jnp.float32)
                for rows in split_rows(hidden_blocks, 2, dp_size)
            ]
        )
        * inv_root
    ).astype(jnp.bfloat16)
    down_parts, down_fetched = lax.optimization_barrier((down_parts, down_fetched))
    down_full = swap_shares(down_fetched, down_blocks)
    grad_down = lax.psum_scatter(
        down_parts, "dp", scatter_dimension=0, tiled=False
    ).astype(jnp.float32)
    grad_down = jnp.transpose(grad_down, (1, 0, 2, 3))
    grad_hidden = jnp.einsum(
        "thso,jhso->thj", picked, down_full, preferred_element_type=jnp.float32
    ).reshape(tokens_here, -1)
    grad_pre = (grad_hidden * slopes).astype(jnp.bfloat16)
    grad_blocks = grad_pre.reshape(tokens_here, hidden_here, block_size)
    up_parts = jnp.stack(
        [
            jnp.einsum("thsi,thj->hsij", rows, grad_blocks, preferred_element_type=jnp.float32)
            for rows in split_rows(selected, 3, dp_size)
        ]
    )
    slot_ids = jnp.arange(blocks_here, dtype=jnp.int32)

    def section_term(which_section):
        spread = jnp.einsum(
            "thj,ihj->thi",
            grad_blocks,
            up_full[:, :, which_section, :],
            preferred_element_type=jnp.float32,
        )
        placing = (up_pattern[:, which_section][:, None] == slot_ids[None, :]).astype(jnp.float32)
        return jnp.einsum("thi,hd->tdi", spread, placing).reshape(tokens_here, width_here)

    own_term = section_term(0)
    for level_bit in range(section_count - 1):
        outgoing = section_term(level_bit + 1).astype(jnp.bfloat16)
        own_term = own_term + swapped(outgoing, "tensor", level_bit).astype(jnp.float32)
    back_part = lax.dot_general(
        grad_pre, low_right, (((1,), (1,)), ((), ())), preferred_element_type=jnp.float32
    )
    back_low = butterfly_sum(back_part, "tensor").astype(jnp.bfloat16)
    grad_input = (
        own_term + jnp.dot(back_low, low_left, preferred_element_type=jnp.float32)
    ).astype(jnp.bfloat16)
    up_parts, _ = lax.optimization_barrier(((up_parts * inv_root).astype(jnp.bfloat16), grad_down))
    grad_up = lax.psum_scatter(up_parts, "dp", scatter_dimension=0, tiled=False).astype(jnp.float32)
    row_part, low_row_part, grad_up = lax.optimization_barrier((back_low, low_sum, grad_up))
    grad_up = jnp.transpose(grad_up, (2, 0, 1, 3))
    grad_left = lax.psum_scatter(
        (
            lax.dot_general(
                row_part, inputs, (((0,), (0,)), ((), ())), preferred_element_type=jnp.float32
            )
            * inv_root
        ).astype(jnp.bfloat16),
        "dp",
        scatter_dimension=0,
        tiled=True,
    ).astype(jnp.float32)
    grad_right = lax.psum_scatter(
        (
            lax.dot_general(
                low_row_part, grad_pre, (((0,), (0,)), ((), ())), preferred_element_type=jnp.float32
            )
            * inv_root
        ).astype(jnp.bfloat16),
        "dp",
        scatter_dimension=0,
        tiled=True,
    ).astype(jnp.float32)
    return (grad_input, grad_up, grad_down, grad_left, grad_right)


def solution(mesh):
    in_specs = (
        P(("groups", "dp"), "tensor"),
        P(("groups", "dp"), "tensor"),
        P("dp", "tensor", None, None),
        P("dp", "tensor", None, None),
        P(None, "tensor"),
        P(None, "tensor"),
        P("tensor", None),
        P("tensor", None),
    )
    out_specs = (
        P(("groups", "dp"), "tensor"),
        P(("groups", "dp"), "tensor", None, None),
        P(("groups", "dp"), "tensor", None, None),
        P(("groups", "dp"), "tensor"),
        P(("groups", "dp"), "tensor"),
    )
    return jax.shard_map(shards, mesh=mesh, in_specs=in_specs, out_specs=out_specs, check_vma=False)
```

profile of v0, /device:TPU:0, one launch (start us, length us, event | category | flops | bytes accessed | tf_op | source)
XLA Modules:
  0.0 487.6 jit_solution(6907615303255987155)
XLA Ops:
  18.0 58.4 %all-gather.5.cloned.1.call-done = bf16[128,16,3,256]{3,1,2,0:T(8,128)(2,1)} async-done(((bf16[32,16,3,256]{3,1,2,0:T(8,128)(2,1)}), bf16[128,16,3,256]{3,1,2,0:T(8,128)(2,1)}) %all-gather.5.cloned.1.call-update) | async-done | bytes 3145744 | tf_op jit(solution)/shard_map/all_gather | solution.py:29
  76.4 4.0 fusion.35
  94.5 4.8 select_bitcast_fusion
  104.8 3.5 collective-permute-done.4
  115.3 4.7 select_bitcast_fusion.3
  120.1 13.4 %collective-permute-done = bf16[3,32,16,3,256]{4,2,3,1,0:T(8,128)(2,1)} collective-permute-done((bf16[3,32,16,3,256]{4,2,3,1,0:T(8,128)(2,1)}, bf16[3,32,16,3,256]{4,2,3,1,0:T(8,128)(2,1)}, u32[]{:S(2)}, u32[]{:S(2)}) %collective-permute-start) | collective-permute-done | bytes 2359328 | tf_op jit(solution)/shard_map/ppermute | solution.py:47
  133.5 3.5 fusion.24
  137.0 4.4 fusion.7
  141.4 11.1 %fusion.8 = f32[16,256,256,1]{2,1,3,0:T(8,128)} fusion(bf16[256,16,3,256]{3,1,2,0:T(8,128)(2,1)S(1)} %bitcast.201, bf16[256,16,1,256]{3,0,2,1:T(8,128)(2,1)} %get-tuple-element.70, bf16[256,16,1,256]{3,0,2,1:T(8,128)(2,1)} %get-tuple-element.71, bf16[256,16,1,256]{3,0,2,1:T(8,128)(2,1)} %select_bitcast_fusion.5), kind=kOutput, calls=%fused_computation.38 | convolution fusion | flops 1616904192 | bytes 16777216 | tf_op jit(solution)/shard_map/thsi,ihsj->thj/dot_general | solution.py:117
  152.5 5.7 %copy.99 = f32[256,4096]{1,0:T(8,128)} copy(f32[256,4096]{0,1:T(8,128)} %bitcast.214) | data formatting | bytes 8388608 | tf_op jit(solution)/shard_map/reshape | solution.py:122
  158.2 6.6 %multiply_convert_fusion = (bf16[256,4096]{1,0:T(8,128)(2,1)}, f32[256,4096]{1,0:T(8,128)}) fusion(f32[256,4096]{1,0:T(8,128)} %copy.99, bf16[256,128]{1,0:T(8,128)(2,1)S(1)} %add_convert_fusion.2, bf16[128,4096]{1,0:T(8,128)(2,1)S(1)} %copy-done), kind=kOutput, calls=%fused_computation.52 | convolution fusion | flops 278921216 | bytes 11599872 | tf_op jit(solution)/shard_map/dot_general | solution.py:122
  164.8 4.2 copy.152
  178.4 4.1 fusion
  186.7 4.8 pad_maximum_fusion
  192.7 44.6 %collective-permute-done.5 = bf16[3,32,16,3,256]{4,2,3,1,0:T(8,128)(2,1)S(1)} collective-permute-done((bf16[3,32,16,3,256]{4,2,3,1,0:T(8,128)(2,1)S(1)}, bf16[3,32,16,3,256]{4,2,3,1,0:T(8,128)(2,1)S(1)}, u32[]{:S(2)}, u32[]{:S(2)}) %collective-permute-start.5) | collective-permute-done | bytes 2359328 | tf_op jit(solution)/shard_map/ppermute | solution.py:47
  240.4 3.6 fusion.4
  244.1 3.4 fusion.68
  247.5 5.8 %copy.143 = f32[256,4096]{1,0:T(8,128)} copy(f32[256,4096]{0,1:T(8,128)} %bitcast.213) | data formatting | bytes 8388608 | tf_op jit(solution)/shard_map/reshape | solution.py:146
  253.3 5.5 %fusion.17 = bf16[256,4096]{1,0:T(8,128)(2,1)S(1)} fusion(f32[256,4096]{1,0:T(8,128)} %copy.143, f32[256,4096]{1,0:T(8,128)} %get-tuple-element.69), kind=kLoop, calls=%fused_computation.51 | loop fusion | flops 19922944 | bytes 10485760 | tf_op jit(solution)/shard_map/convert_element_type | solution.py:147
  269.9 4.1 fusion.1
  274.0 18.3 %reduce-scatter.5.cloned.1.call-done = bf16[1,16,64,3,256]{4,2,3,1,0:T(8,128)(2,1)} async-done(((bf16[4,16,64,3,256]{4,2,3,1,0:T(8,128)(2,1)}), bf16[1,16,64,3,256]{4,2,3,1,0:T(8,128)(2,1)}) %reduce-scatter.5.cloned.1.call-update) | async-done | bytes 1572880 | tf_op jit(solution)/shard_map/reduce_scatter | solution.py:140
  292.2 3.5 convert_bitcast_fusion
  301.0 4.1 collective-permute-done.9
  305.1 102.1 %reduce-scatter.7.cloned.1.call-done = bf16[1,16,3,64,256]{4,3,2,1,0:T(8,128)(2,1)} async-done(((bf16[4,16,3,64,256]{4,3,2,1,0:T(8,128)(2,1)}), bf16[1,16,3,64,256]{4,3,2,1,0:T(8,128)(2,1)}) %reduce-scatter.7.cloned.1.call-update) | async-done | bytes 1572880 | tf_op jit(solution)/shard_map/reduce_scatter | solution.py:179
  407.2 3.6 bitcast_convert_fusion
  412.1 5.4 %fusion.69 = (bf16[256,16,1,256]{3,1,2,0:T(8,128)(2,1)S(1)}, bf16[256,16,1,256]{3,1,2,0:T(8,128)(2,1)}, bf16[256,16,1,256]{3,1,2,0:T(8,128)(2,1)}) fusion(bf16[256,16,3,256]{3,1,2,0:T(8,128)(2,1)} %bitcast.202), kind=kLoop, calls=%fused_computation.151 | loop fusion | bytes 12582912 | tf_op jit(solution)/shard_map/slice | solution.py:161
  419.9 4.5 copy.115
  429.3 3.9 convolution_bitcast_fusion
  433.2 4.5 copy.118
  449.7 17.4 %collective-permute-done.7 = bf16[256,2048]{1,0:T(8,128)(2,1)} collective-permute-done((bf16[256,2048]{1,0:T(8,128)(2,1)}, bf16[256,2048]{1,0:T(8,128)(2,1)}, u32[]{:S(2)}, u32[]{:S(2)}) %collective-permute-start.7) | collective-permute-done | bytes 1048608 | tf_op jit(solution)/shard_map/ppermute | solution.py:19
  470.1 3.5 copy.128
  473.6 3.5 copy.127
  (151 shorter events, 98.1 us)
Async XLA Ops:
  7.2 151.0 %copy-start = (bf16[128,4096]{1,0:T(8,128)(2,1)S(1)}, bf16[128,4096]{1,0:T(8,128)(2,1)}, u32[]{:S(2)}) copy-start(bf16[128,4096]{1,0:T(8,128)(2,1)} %param.15) | copy-start | bytes 3145732
  7.2 7.2 %copy-start.20 = (bf16[128,2048]{1,0:T(8,128)(2,1)S(1)}, bf16[128,2048]{1,0:T(8,128)(2,1)}, u32[]{:S(2)}) copy-start(bf16[128,2048]{1,0:T(8,128)(2,1)} %param.14) | copy-start | bytes 1572868
  7.2 69.2 %all-gather.5.cloned.1.call-start = ((), (), s32[]{:S(2)}) async-start(), calls=%async_computation.8 | async-start | bytes 3932160 | tf_op jit(solution)/shard_map/all_gather | solution.py:29
  10.1 172.4 %all-gather.7.cloned.1.call-start = ((), (), s32[]{:S(2)}) async-start(), calls=%async_computation.9 | async-start | bytes 3932160 | tf_op jit(solution)/shard_map/all_gather | solution.py:29
  11.5 6.5 %copy-start.28 = (s32[16,3]{0,1:T(4,128)S(1)}, s32[16,3]{0,1:T(4,128)}, u32[]{:S(2)}) copy-start(s32[16,3]{0,1:T(4,128)} %param.17) | copy-start | bytes 580
  11.5 96.9 %collective-permute-start.1 = (bf16[256,2048]{0,1:T(8,128)(2,1)}, bf16[256,2048]{0,1:T(8,128)(2,1)}, u32[]{:S(2)}, u32[]{:S(2)}) collective-permute-start(bf16[256,2048]{0,1:T(8,128)(2,1)} %copy.92), channel_id=1, source_target_pairs={{0,1},{1,0},{2,3},{3,2},{4,5},{5,4},{6,7},{7,6},{8,9},{9,8},{10,11... | collective-permute-start | bytes 3145736 | tf_op jit(solution)/shard_map/ppermute | solution.py:19
  11.9 97.9 %collective-permute-start.2 = (bf16[256,2048]{0,1:T(8,128)(2,1)}, bf16[256,2048]{0,1:T(8,128)(2,1)}, u32[]{:S(2)}, u32[]{:S(2)}) collective-permute-start(bf16[256,2048]{0,1:T(8,128)(2,1)} %copy.92), channel_id=1, source_target_pairs={{0,2},{2,0},{1,3},{3,1},{4,6},{6,4},{5,7},{7,5},{8,10},{10,8},{9,1... | collective-permute-start | bytes 3145736 | tf_op jit(solution)/shard_map/ppermute | solution.py:19
  14.9 88.5 %collective-permute-start.3 = (f32[256,128]{1,0:T(8,128)S(1)}, f32[256,128]{1,0:T(8,128)S(1)}, u32[]{:S(2)}, u32[]{:S(2)}) collective-permute-start(f32[256,128]{1,0:T(8,128)S(1)} %fusion.70), channel_id=1, source_target_pairs={{0,1},{1,0},{2,3},{3,2},{4,5},{5,4},{6,7},{7,6},{8,9},{9,8},{10,11... | collective-permute-start | bytes 393224 | tf_op jit(solution)/shard_map/ppermute | solution.py:19
  17.8 274.4 %reduce-scatter.5.cloned.1.call-start = ((), (), s32[]{:S(2)}) async-start(), calls=%async_computation.4 | async-start | bytes 7864320 | tf_op jit(solution)/shard_map/reduce_scatter | solution.py:140
  76.4 7.2 %copy-start.26 = (bf16[256,2048]{1,0:T(8,128)(2,1)S(1)}, bf16[256,2048]{1,0:T(8,128)(2,1)}, u32[]{:S(2)}) copy-start(bf16[256,2048]{1,0:T(8,128)(2,1)} %param.11) | copy-start | bytes 3145732
  80.4 53.1 %collective-permute-start = (bf16[3,32,16,3,256]{4,2,3,1,0:T(8,128)(2,1)}, bf16[3,32,16,3,256]{4,2,3,1,0:T(8,128)(2,1)}, u32[]{:S(2)}, u32[]{:S(2)}) collective-permute-start(bf16[3,32,16,3,256]{4,2,3,1,0:T(8,128)(2,1)} %fusion.35), channel_id=1, source_target_pairs={{0,16},{16,0},{1,17},{17,1},{2,18},{18,2},{3,19},{19,3},{4,20},{20... | collective-permute-start | bytes 7077896 | tf_op jit(solution)/shard_map/ppermute | solution.py:47
  94.5 4.9 copy-start.13
  103.3 5.0 %collective-permute-start.4 = (f32[256,128]{1,0:T(8,128)S(1)}, f32[256,128]{1,0:T(8,128)S(1)}, u32[]{:S(2)}, u32[]{:S(2)}) collective-permute-start(f32[256,128]{1,0:T(8,128)S(1)} %add.90), channel_id=1, source_target_pairs={{0,2},{2,0},{1,3},{3,1},{4,6},{6,4},{5,7},{7,5},{8,10},{10,8},{9,1... | collective-permute-start | bytes 393224 | tf_op jit(solution)/shard_map/ppermute | solution.py:19
  115.3 18.2 %copy-start.15 = (bf16[1,32,16,3,256]{4,2,3,1,0:T(8,128)(2,1)S(1)}, bf16[1,32,16,3,256]{4,2,3,1,0:T(8,128)(2,1)}, u32[]{:S(2)}) copy-start(bf16[1,32,16,3,256]{4,2,3,1,0:T(8,128)(2,1)} %get-tuple-element.55) | copy-start | bytes 2359300
  141.4 11.1 %copy-start.3 = (bf16[4,2,32,16,3,256]{5,3,4,2,1,0:T(8,128)(2,1)}, bf16[4,2,32,16,3,256]{5,3,4,2,1,0:T(8,128)(2,1)S(1)}, u32[]{:S(2)}) copy-start(bf16[4,2,32,16,3,256]{5,3,4,2,1,0:T(8,128)(2,1)S(1)} %fusion.7) | copy-start | bytes 18874372
  169.0 4.3 copy-start.24
  182.5 4.3 copy-start.10
  182.5 224.7 %reduce-scatter.7.cloned.1.call-start = ((), (), s32[]{:S(2)}) async-start(), calls=%async_computation.5 | async-start | bytes 7864320 | tf_op jit(solution)/shard_map/reduce_scatter | solution.py:179
  185.2 6.4 %copy-start.6 = (bf16[128,16,3,256]{3,1,2,0:T(8,128)(2,1)S(1)}, bf16[128,16,3,256]{3,1,2,0:T(8,128)(2,1)}, u32[]{:S(2)}) copy-start(bf16[128,16,3,256]{3,1,2,0:T(8,128)(2,1)} %all-gather.7.cloned.1.call-done) | copy-start | bytes 9437188
  185.2 52.0 %collective-permute-start.5 = (bf16[3,32,16,3,256]{4,2,3,1,0:T(8,128)(2,1)S(1)}, bf16[3,32,16,3,256]{4,2,3,1,0:T(8,128)(2,1)S(1)}, u32[]{:S(2)}, u32[]{:S(2)}) collective-permute-start(bf16[3,32,16,3,256]{4,2,3,1,0:T(8,128)(2,1)S(1)} %fusion.34), channel_id=1, source_target_pairs={{0,16},{16,0},{1,17},{17,1},{2,18},{18,2},{3,19},{19,3},{4,20},{20... | collective-permute-start | bytes 7077896 | tf_op jit(solution)/shard_map/ppermute | solution.py:47
  191.6 45.7 %copy-start.14 = (bf16[1,32,16,3,256]{4,2,3,1,0:T(8,128)(2,1)S(1)}, bf16[1,32,16,3,256]{4,2,3,1,0:T(8,128)(2,1)}, u32[]{:S(2)}) copy-start(bf16[1,32,16,3,256]{4,2,3,1,0:T(8,128)(2,1)} %get-tuple-element.53) | copy-start | bytes 2359300
  247.5 13.3 %slice-start = ((s8[6291456]{0:T(1024)(128)(4,1)}), s8[2097152]{0:T(1024)(128)(4,1)S(1)}, s32[]{:S(2)}) async-start(s8[6291456]{0:T(1024)(128)(4,1)} %bitcast.191), calls=%async_computation.10 | async-start | bytes 4194304
  253.3 7.5 %slice-start.1 = ((s8[6291456]{0:T(1024)(128)(4,1)}), s8[4194304]{0:T(1024)(128)(4,1)S(1)}, s32[]{:S(2)}) async-start(s8[6291456]{0:T(1024)(128)(4,1)} %bitcast.191), calls=%async_computation.11 | async-start | bytes 8388608
  295.7 181.4 %reduce-scatter.9.cloned.1.call-start = ((), (), s32[]{:S(2)}) async-start(), calls=%async_computation.6 | async-start | bytes 655360 | tf_op jit(solution)/shard_map/reduce_scatter | solution.py:182
  298.0 1.4 collective-permute-start.8
  299.4 5.6 %collective-permute-start.9 = (f32[256,128]{1,0:T(8,128)S(1)}, f32[256,128]{1,0:T(8,128)S(1)}, u32[]{:S(2)}, u32[]{:S(2)}) collective-permute-start(f32[256,128]{1,0:T(8,128)S(1)} %add.99), channel_id=1, source_target_pairs={{0,2},{2,0},{1,3},{3,1},{4,6},{6,4},{5,7},{7,5},{8,10},{10,8},{9,1... | collective-permute-start | bytes 393224 | tf_op jit(solution)/shard_map/ppermute | solution.py:19
  411.9 66.8 %reduce-scatter.11.cloned.1.call-start = ((), (), s32[]{:S(2)}) async-start(), calls=%async_computation.7 | async-start | bytes 1310720 | tf_op jit(solution)/shard_map/reduce_scatter | solution.py:193
  427.8 21.9 %collective-permute-start.6 = (bf16[256,2048]{1,0:T(8,128)(2,1)}, bf16[256,2048]{1,0:T(8,128)(2,1)}, u32[]{:S(2)}, u32[]{:S(2)}) collective-permute-start(bf16[256,2048]{1,0:T(8,128)(2,1)} %bitcast.98), channel_id=1, source_target_pairs={{0,1},{1,0},{2,3},{3,2},{4,5},{5,4},{6,7},{7,6},{8,9},{9,8},{10,11... | collective-permute-start | bytes 3145736 | tf_op jit(solution)/shard_map/ppermute | solution.py:19
  437.7 4.9 %copy-start.25 = (bf16[256,16,1,256]{3,1,2,0:T(8,128)(2,1)S(1)}, bf16[256,16,1,256]{3,1,2,0:T(8,128)(2,1)}, u32[]{:S(2)}) copy-start(bf16[256,16,1,256]{3,1,2,0:T(8,128)(2,1)} %get-tuple-element.51) | copy-start | bytes 6291460
  441.2 25.9 %collective-permute-start.7 = (bf16[256,2048]{1,0:T(8,128)(2,1)}, bf16[256,2048]{1,0:T(8,128)(2,1)}, u32[]{:S(2)}, u32[]{:S(2)}) collective-permute-start(bf16[256,2048]{1,0:T(8,128)(2,1)} %bitcast.100), channel_id=1, source_target_pairs={{0,2},{2,0},{1,3},{3,1},{4,6},{6,4},{5,7},{7,5},{8,10},{10,8},{9,1... | collective-permute-start | bytes 3145736 | tf_op jit(solution)/shard_map/ppermute | solution.py:19
  448.8 18.3 %copy-start.21 = (bf16[128,2048]{1,0:T(8,128)(2,1)S(1)}, bf16[128,2048]{1,0:T(8,128)(2,1)}, u32[]{:S(2)}) copy-start(bf16[128,2048]{1,0:T(8,128)(2,1)} %param.14) | copy-start | bytes 1572868
  449.7 20.5 %copy-start.4 = (f32[64,16,3,256]{3,0,2,1:T(8,128)S(1)}, f32[64,16,3,256]{3,0,2,1:T(8,128)}, u32[]{:S(2)}) copy-start(f32[64,16,3,256]{3,0,2,1:T(8,128)} %convert_bitcast_fusion) | copy-start | bytes 9437188
  (15 other events, 47.1 us)
Sparse Core Ops, SparseCore 0:
  10.2 66.1 all-gather.4
  77.9 62.0 all-gather.6
  182.6 109.6 reduce-scatter.4
  295.9 111.2 reduce-scatter.6
  412.0 22.3 reduce-scatter.8
  436.6 25.5 reduce-scatter.10
where the time goes:
time: 491 us; the launch traced here: 488 us
  waiting for transfers between devices  263 us (54%)
  local copies, waits for them, and re-layouts  77.9 us (16%)
  other arithmetic  62.1 us (13%)
  matrix products  58.2 us (12%)
  between operations  14.9 us (3%)
  starting transfers between devices  11.3 us (2%)
    reduce_scatter x1, waiting for transfers between devices, shards(): lax.psum_scatter(up_parts, 'dp', scatter_dimension=0, tiled=False)  102 us
    all_gather x2, waiting for transfers between devices, fetch_share(): return lax.all_gather(mine, 'dp', axis=0, tiled=False)  58.4 us
    ppermute x2, waiting for transfers between devices, swap_shares(): got = lax.ppermute(send, 'groups', [(0, 1), (1, 0)])  58 us
    ppermute x8, waiting for transfers between devices, swapped(): return lax.ppermute(block, axis, route)  26.3 us
    unnamed x70, local copies, waits for them, and re-layouts  18.5 us
    reduce_scatter x1, waiting for transfers between devices, shards(): lax.psum_scatter(down_parts, 'dp', scatter_dimension=0, tiled=False)  18.3 us
    another operation x5, other arithmetic, pick_blocks(): return jnp.stack(picked, axis=2)  17.7 us
    transpose x3, local copies, waits for them, and re-layouts, section_term(): jnp.einsum('thj,ihj->thi', grad_blocks, up_full[:, :, which_section, :],...  12.4 us
  transfers between devices with their start and end apart: 16, of which 9 were waited for; matrix products, arithmetic and copies ran while one was open for 37% of the time, Pallas kernels for 0%

commit v1 on v0

--- a/solution.py
+++ b/solution.py
@@ -164,10 +164,16 @@
         placing = (up_pattern[:, which_section][:, None] == slot_ids[None, :]).astype(jnp.float32)
         return jnp.einsum("thi,hd->tdi", spread, placing).reshape(tokens_here, width_here)
 
+    incoming = [
+        swapped(section_term(level_bit + 1).astype(jnp.bfloat16), "tensor", level_bit)
+        for level_bit in range(section_count - 1)
+    ]
+    up_parts, incoming, _ = lax.optimization_barrier(
+        ((up_parts * inv_root).astype(jnp.bfloat16), incoming, grad_down)
+    )
     own_term = section_term(0)
     for level_bit in range(section_count - 1):
-        outgoing = section_term(level_bit + 1).astype(jnp.bfloat16)
-        own_term = own_term + swapped(outgoing, "tensor", level_bit).astype(jnp.float32)
+        own_term = own_term + incoming[level_bit].astype(jnp.float32)
     back_part = lax.dot_general(
         grad_pre, low_right, (((1,), (1,)), ((), ())), preferred_element_type=jnp.float32
     )
@@ -175,32 +181,31 @@
     grad_input = (
         own_term + jnp.dot(back_low, low_left, preferred_element_type=jnp.float32)
     ).astype(jnp.bfloat16)
-    up_parts, _ = lax.optimization_barrier(((up_parts * inv_root).astype(jnp.bfloat16), grad_down))
     grad_up = lax.psum_scatter(up_parts, "dp", scatter_dimension=0, tiled=False).astype(jnp.float32)
     row_part, low_row_part, grad_up = lax.optimization_barrier((back_low, low_sum, grad_up))
     grad_up = jnp.transpose(grad_up, (2, 0, 1, 3))
-    grad_left = lax.psum_scatter(
-        (
+    left_parts = jnp.stack(
+        split_rows(
             lax.dot_general(
                 row_part, inputs, (((0,), (0,)), ((), ())), preferred_element_type=jnp.float32
-            )
-            * inv_root
-        ).astype(jnp.bfloat16),
-        "dp",
-        scatter_dimension=0,
-        tiled=True,
-    ).astype(jnp.float32)
-    grad_right = lax.psum_scatter(
-        (
+            ),
+            0,
+            dp_size,
+        )
+    )
+    right_parts = jnp.stack(
+        split_rows(
             lax.dot_general(
                 low_row_part, grad_pre, (((0,), (0,)), ((), ())), preferred_element_type=jnp.float32
-            )
-            * inv_root
-        ).astype(jnp.bfloat16),
-        "dp",
-        scatter_dimension=0,
-        tiled=True,
-    ).astype(jnp.float32)
+            ),
+            0,
+            dp_size,
+        )
+    )
+    joined = (jnp.concatenate([left_parts, right_parts], axis=2) * inv_root).astype(jnp.bfloat16)
+    joined = lax.psum_scatter(joined, "dp", scatter_dimension=0, tiled=False).astype(jnp.float32)
+    grad_left = joined[:, :width_here]
+    grad_right = joined[:, width_here:]
     return (grad_input, grad_up, grad_down, grad_left, grad_right)
 
 

time: 491 us -> 471 us (0.959)
  waiting for transfers between devices: 263 us -> 246 us
    reduce_scatter x1, waiting for transfers between devices: 18.3 us -> 0.01 us  [shards(): lax.psum_scatter(down_parts, 'dp', scatter_dimension=0, tiled=False)]
    reduce_scatter x2 -> x1, waiting for transfers between devices: 0.01 us -> 16.2 us  [shards(): lax.psum_scatter(joined, 'dp', scatter_dimension=0, tiled=False)]
    ppermute x8, waiting for transfers between devices: 26.3 us -> 16.2 us  [swapped(): return lax.ppermute(block, axis, route)]
    ppermute x2, waiting for transfers between devices: 58 us -> 53 us  [swap_shares(): got = lax.ppermute(send, 'groups', [(0, 1), (1, 0)])]
    unnamed x70 -> x76, local copies, waits for them, and re-layouts: 18.5 us -> 17.7 us
  transfers between devices with their start and end apart: 16 -> 15, of which waited for: 9 -> 9; matrix products, arithmetic and copies ran while one was open for 37% -> 39% of each run, Pallas kernels for 0% -> 0%
where the time goes in v1:
time: 471 us; the launch traced here: 468 us
  waiting for transfers between devices  246 us (52%)
  local copies, waits for them, and re-layouts  76.5 us (16%)
  other arithmetic  62.1 us (13%)
  matrix products  57 us (12%)
  between operations  14.7 us (3%)
  starting transfers between devices  11.3 us (2%)
    reduce_scatter x1, waiting for transfers between devices, shards(): lax.psum_scatter(up_parts, 'dp', scatter_dimension=0, tiled=False)  102 us
    all_gather x2, waiting for transfers between devices, fetch_share(): return lax.all_gather(mine, 'dp', axis=0, tiled=False)  58.4 us
    ppermute x2, waiting for transfers between devices, swap_shares(): got = lax.ppermute(send, 'groups', [(0, 1), (1, 0)])  53 us
    another operation x5, other arithmetic, pick_blocks(): return jnp.stack(picked, axis=2)  19.6 us
    unnamed x76, local copies, waits for them, and re-layouts  17.7 us
    reduce_scatter x1, waiting for transfers between devices, shards(): lax.psum_scatter(joined, 'dp', scatter_dimension=0, tiled=False)  16.2 us
    ppermute x8, waiting for transfers between devices, swapped(): return lax.ppermute(block, axis, route)  16.2 us
    transpose x3, local copies, waits for them, and re-layouts, section_term(): jnp.einsum('thj,ihj->thi', grad_blocks, up_full[:, :, which_section, :],...  12.8 us
  transfers between devices with their start and end apart: 15, of which 9 were waited for; matrix products, arithmetic and copies ran while one was open for 39% of the time, Pallas kernels for 0%

profile of v1, /device:TPU:0, one launch (start us, length us, event | category | flops | bytes accessed | tf_op | source)
XLA Modules:
  0.0 467.5 jit_solution(7534521673296140730)
XLA Ops:
  17.9 58.4 %all-gather.5.cloned.1.call-done = bf16[128,16,3,256]{3,1,2,0:T(8,128)(2,1)} async-done(((bf16[32,16,3,256]{3,1,2,0:T(8,128)(2,1)}), bf16[128,16,3,256]{3,1,2,0:T(8,128)(2,1)}) %all-gather.5.cloned.1.call-update) | async-done | bytes 3145744 | tf_op jit(solution)/shard_map/all_gather | solution.py:29
  76.4 4.0 fusion.34
  94.5 4.9 %select_bitcast_fusion = (bf16[256,16,1,256]{3,0,2,1:T(8,128)(2,1)}, bf16[256,16,1,256]{3,0,2,1:T(8,128)(2,1)}) fusion(bf16[16,256,256]{2,1,0:T(8,128)(2,1)} %gather_fusion.5, pred[16]{0:T(512)(128)(4,1)S(1)} %get-tuple-element.72, bf16[16,256,256]{2,1,0:T(8,128)(2,1)} %gather_fusion.4, pred[16]{0:T(512)(128)(4,1)S(1)} %get-tuple-element.74), kind=kLoop, calls=%fused_computation.82 | loop fusion | flops 2097152 | bytes 8388640 | tf_op jit(solution)/shard_map/stack | solution.py:97
  104.9 3.5 collective-permute-done.4
  115.5 4.8 %select_bitcast_fusion.3 = (bf16[256,16,1,256]{3,0,2,1:T(8,128)(2,1)}, bf16[256,16,1,256]{3,0,2,1:T(8,128)(2,1)}) fusion(bf16[16,256,256]{2,1,0:T(8,128)(2,1)} %gather_fusion.2, pred[16]{0:T(512)(128)(4,1)S(1)} %get-tuple-element.76, bf16[16,256,256]{2,1,0:T(8,128)(2,1)} %gather_fusion.1, pred[16]{0:T(512)(128)(4,1)S(1)} %get-tuple-element.78), kind=kLoop, calls=%fused_computation.85 | loop fusion | flops 2097152 | bytes 8388640 | tf_op jit(solution)/shard_map/stack | solution.py:97
  120.3 13.2 %collective-permute-done = bf16[3,32,16,3,256]{4,2,3,1,0:T(8,128)(2,1)} collective-permute-done((bf16[3,32,16,3,256]{4,2,3,1,0:T(8,128)(2,1)}, bf16[3,32,16,3,256]{4,2,3,1,0:T(8,128)(2,1)}, u32[]{:S(2)}, u32[]{:S(2)}) %collective-permute-start) | collective-permute-done | bytes 2359328 | tf_op jit(solution)/shard_map/ppermute | solution.py:47
  133.5 3.5 fusion.23
  137.0 4.4 fusion.7
  141.4 11.1 %fusion.8 = f32[16,256,256,1]{2,1,3,0:T(8,128)} fusion(bf16[256,16,3,256]{3,1,2,0:T(8,128)(2,1)S(1)} %bitcast.220, bf16[256,16,1,256]{3,0,2,1:T(8,128)(2,1)} %get-tuple-element.82, bf16[256,16,1,256]{3,0,2,1:T(8,128)(2,1)} %get-tuple-element.83, bf16[256,16,1,256]{3,0,2,1:T(8,128)(2,1)} %select_bitcast_fusion.5), kind=kOutput, calls=%fused_computation.38 | convolution fusion | flops 1616904192 | bytes 16777216 | tf_op jit(solution)/shard_map/thsi,ihsj->thj/dot_general | solution.py:117
  152.5 5.7 %copy.99 = f32[256,4096]{1,0:T(8,128)} copy(f32[256,4096]{0,1:T(8,128)} %bitcast.235) | data formatting | bytes 8388608 | tf_op jit(solution)/shard_map/reshape | solution.py:122
  158.2 6.6 %multiply_convert_fusion = (bf16[256,4096]{1,0:T(8,128)(2,1)}, f32[256,4096]{1,0:T(8,128)}) fusion(f32[256,4096]{1,0:T(8,128)} %copy.99, bf16[256,128]{1,0:T(8,128)(2,1)S(1)} %add_convert_fusion.2, bf16[128,4096]{1,0:T(8,128)(2,1)S(1)} %copy-done), kind=kOutput, calls=%fused_computation.50 | convolution fusion | flops 278921216 | bytes 11599872 | tf_op jit(solution)/shard_map/dot_general | solution.py:122
  164.8 4.2 copy.152
  178.6 3.9 fusion
  186.8 6.7 %pad_maximum_fusion = bf16[256,16,3,256]{3,0,2,1:T(8,128)(2,1)} fusion(bf16[256,16,1,256]{3,0,2,1:T(8,128)(2,1)S(1)} %copy-done.11, bf16[256,16,1,256]{3,0,2,1:T(8,128)(2,1)} %get-tuple-element.83, bf16[256,16,1,256]{3,0,2,1:T(8,128)(2,1)} %select_bitcast_fusion.5), kind=kLoop, calls=%fused_computation.30 | loop fusion | flops 6291456 | bytes 12582912 | tf_op jit(solution)/shard_map/stack | solution.py:97
  197.4 39.8 %collective-permute-done.5 = bf16[3,32,16,3,256]{4,2,3,1,0:T(8,128)(2,1)S(1)} collective-permute-done((bf16[3,32,16,3,256]{4,2,3,1,0:T(8,128)(2,1)S(1)}, bf16[3,32,16,3,256]{4,2,3,1,0:T(8,128)(2,1)S(1)}, u32[]{:S(2)}, u32[]{:S(2)}) %collective-permute-start.5) | collective-permute-done | bytes 2359328 | tf_op jit(solution)/shard_map/ppermute | solution.py:47
  240.4 3.6 fusion.4
  244.1 3.4 fusion.67
  247.5 5.7 %copy.143 = f32[256,4096]{1,0:T(8,128)} copy(f32[256,4096]{0,1:T(8,128)} %bitcast.234) | data formatting | bytes 8388608 | tf_op jit(solution)/shard_map/reshape | solution.py:146
  253.2 5.0 %fusion.16 = bf16[256,4096]{1,0:T(8,128)(2,1)S(1)} fusion(f32[256,4096]{1,0:T(8,128)} %copy.143, f32[256,4096]{1,0:T(8,128)} %get-tuple-element.81), kind=kLoop, calls=%fused_computation.49 | loop fusion | flops 19922944 | bytes 10485760 | tf_op jit(solution)/shard_map/convert_element_type | solution.py:147
  260.6 4.6 copy.123
  270.9 4.8 %copy.126 = bf16[256,16,256]{2,1,0:T(8,128)(2,1)} copy(bf16[256,16,256]{0,2,1:T(8,128)(2,1)} %convolution_bitcast_fusion) | data formatting | bytes 4194304 | tf_op jit(solution)/shard_map/thj,ihj->thi/transpose | solution.py:158
  290.4 3.9 fusion.1
  294.3 3.5 convert_bitcast_fusion
  297.8 7.3 %collective-permute-done.7 = bf16[256,2048]{1,0:T(8,128)(2,1)} collective-permute-done((bf16[256,2048]{1,0:T(8,128)(2,1)}, bf16[256,2048]{1,0:T(8,128)(2,1)}, u32[]{:S(2)}, u32[]{:S(2)}) %collective-permute-start.7) | collective-permute-done | bytes 1048608 | tf_op jit(solution)/shard_map/ppermute | solution.py:19
  309.1 4.0 collective-permute-done.9
  313.1 102.1 %reduce-scatter.6.cloned.1.call-done = bf16[1,16,3,64,256]{4,3,2,1,0:T(8,128)(2,1)} async-done(((bf16[4,16,3,64,256]{4,3,2,1,0:T(8,128)(2,1)}), bf16[1,16,3,64,256]{4,3,2,1,0:T(8,128)(2,1)}) %reduce-scatter.6.cloned.1.call-update) | async-done | bytes 1572880 | tf_op jit(solution)/shard_map/reduce_scatter | solution.py:184
  415.2 3.5 bitcast_convert_fusion
  422.1 3.9 convolution_bitcast_fusion.2
  426.0 3.4 copy.112
  431.7 3.5 copy.128
  438.4 3.5 copy.127
  441.9 16.2 %reduce-scatter.8.cloned.1.call-done = bf16[1,32,6144]{2,1,0:T(8,128)(2,1)} async-done(((bf16[4,32,6144]{2,1,0:T(8,128)(2,1)}), bf16[1,32,6144]{2,1,0:T(8,128)(2,1)}) %reduce-scatter.8.cloned.1.call-update) | async-done | bytes 393232 | tf_op jit(solution)/shard_map/reduce_scatter | solution.py:206
  (159 shorter events, 96.2 us)
Async XLA Ops:
  7.2 151.0 %copy-start = (bf16[128,4096]{1,0:T(8,128)(2,1)S(1)}, bf16[128,4096]{1,0:T(8,128)(2,1)}, u32[]{:S(2)}) copy-start(bf16[128,4096]{1,0:T(8,128)(2,1)} %param.15) | copy-start | bytes 3145732
  7.2 7.2 %copy-start.20 = (bf16[128,2048]{1,0:T(8,128)(2,1)S(1)}, bf16[128,2048]{1,0:T(8,128)(2,1)}, u32[]{:S(2)}) copy-start(bf16[128,2048]{1,0:T(8,128)(2,1)} %param.14) | copy-start | bytes 1572868
  7.2 69.2 %all-gather.5.cloned.1.call-start = ((), (), s32[]{:S(2)}) async-start(), calls=%async_computation.6 | async-start | bytes 3932160 | tf_op jit(solution)/shard_map/all_gather | solution.py:29
  10.1 172.4 %all-gather.7.cloned.1.call-start = ((), (), s32[]{:S(2)}) async-start(), calls=%async_computation.7 | async-start | bytes 3932160 | tf_op jit(solution)/shard_map/all_gather | solution.py:29
  11.4 6.4 %copy-start.29 = (s32[16,3]{0,1:T(4,128)S(1)}, s32[16,3]{0,1:T(4,128)}, u32[]{:S(2)}) copy-start(s32[16,3]{0,1:T(4,128)} %param.17) | copy-start | bytes 580
  11.4 97.0 %collective-permute-start.1 = (bf16[256,2048]{0,1:T(8,128)(2,1)}, bf16[256,2048]{0,1:T(8,128)(2,1)}, u32[]{:S(2)}, u32[]{:S(2)}) collective-permute-start(bf16[256,2048]{0,1:T(8,128)(2,1)} %copy.92), channel_id=1, source_target_pairs={{0,1},{1,0},{2,3},{3,2},{4,5},{5,4},{6,7},{7,6},{8,9},{9,8},{10,11... | collective-permute-start | bytes 3145736 | tf_op jit(solution)/shard_map/ppermute | solution.py:19
  11.9 98.0 %collective-permute-start.2 = (bf16[256,2048]{0,1:T(8,128)(2,1)}, bf16[256,2048]{0,1:T(8,128)(2,1)}, u32[]{:S(2)}, u32[]{:S(2)}) collective-permute-start(bf16[256,2048]{0,1:T(8,128)(2,1)} %copy.92), channel_id=1, source_target_pairs={{0,2},{2,0},{1,3},{3,1},{4,6},{6,4},{5,7},{7,5},{8,10},{10,8},{9,1... | collective-permute-start | bytes 3145736 | tf_op jit(solution)/shard_map/ppermute | solution.py:19
  14.9 88.5 %collective-permute-start.3 = (f32[256,128]{1,0:T(8,128)S(1)}, f32[256,128]{1,0:T(8,128)S(1)}, u32[]{:S(2)}, u32[]{:S(2)}) collective-permute-start(f32[256,128]{1,0:T(8,128)S(1)} %fusion.69), channel_id=1, source_target_pairs={{0,1},{1,0},{2,3},{3,2},{4,5},{5,4},{6,7},{7,6},{8,9},{9,8},{10,11... | collective-permute-start | bytes 393224 | tf_op jit(solution)/shard_map/ppermute | solution.py:19
  17.8 276.5 %reduce-scatter.4.cloned.1.call-start = ((), (), s32[]{:S(2)}) async-start(), calls=%async_computation.3 | async-start | bytes 7864320 | tf_op jit(solution)/shard_map/reduce_scatter | solution.py:140
  76.4 7.2 %copy-start.27 = (bf16[256,2048]{1,0:T(8,128)(2,1)S(1)}, bf16[256,2048]{1,0:T(8,128)(2,1)}, u32[]{:S(2)}) copy-start(bf16[256,2048]{1,0:T(8,128)(2,1)} %param.11) | copy-start | bytes 3145732
  80.4 53.1 %collective-permute-start = (bf16[3,32,16,3,256]{4,2,3,1,0:T(8,128)(2,1)}, bf16[3,32,16,3,256]{4,2,3,1,0:T(8,128)(2,1)}, u32[]{:S(2)}, u32[]{:S(2)}) collective-permute-start(bf16[3,32,16,3,256]{4,2,3,1,0:T(8,128)(2,1)} %fusion.34), channel_id=1, source_target_pairs={{0,16},{16,0},{1,17},{17,1},{2,18},{18,2},{3,19},{19,3},{4,20},{20... | collective-permute-start | bytes 7077896 | tf_op jit(solution)/shard_map/ppermute | solution.py:47
  94.5 4.9 %copy-start.13 = (bf16[16,256,256]{2,1,0:T(8,128)(2,1)S(1)}, bf16[16,256,256]{2,1,0:T(8,128)(2,1)}, u32[]{:S(2)}) copy-start(bf16[16,256,256]{2,1,0:T(8,128)(2,1)} %gather_fusion) | copy-start | bytes 6291460
  103.4 5.0 %collective-permute-start.4 = (f32[256,128]{1,0:T(8,128)S(1)}, f32[256,128]{1,0:T(8,128)S(1)}, u32[]{:S(2)}, u32[]{:S(2)}) collective-permute-start(f32[256,128]{1,0:T(8,128)S(1)} %add.88), channel_id=1, source_target_pairs={{0,2},{2,0},{1,3},{3,1},{4,6},{6,4},{5,7},{7,5},{8,10},{10,8},{9,1... | collective-permute-start | bytes 393224 | tf_op jit(solution)/shard_map/ppermute | solution.py:19
  115.5 18.0 %copy-start.15 = (bf16[1,32,16,3,256]{4,2,3,1,0:T(8,128)(2,1)S(1)}, bf16[1,32,16,3,256]{4,2,3,1,0:T(8,128)(2,1)}, u32[]{:S(2)}) copy-start(bf16[1,32,16,3,256]{4,2,3,1,0:T(8,128)(2,1)} %get-tuple-element.63) | copy-start | bytes 2359300
  141.4 11.1 %copy-start.4 = (bf16[4,2,32,16,3,256]{5,3,4,2,1,0:T(8,128)(2,1)}, bf16[4,2,32,16,3,256]{5,3,4,2,1,0:T(8,128)(2,1)S(1)}, u32[]{:S(2)}) copy-start(bf16[4,2,32,16,3,256]{5,3,4,2,1,0:T(8,128)(2,1)S(1)} %fusion.7) | copy-start | bytes 18874372
  182.5 232.7 %reduce-scatter.6.cloned.1.call-start = ((), (), s32[]{:S(2)}) async-start(), calls=%async_computation.4 | async-start | bytes 7864320 | tf_op jit(solution)/shard_map/reduce_scatter | solution.py:184
  182.5 12.0 %slice-start.2 = ((s8[6291456]{0:T(1024)(128)(4,1)}), s8[4194304]{0:T(1024)(128)(4,1)S(1)}, s32[]{:S(2)}) async-start(s8[6291456]{0:T(1024)(128)(4,1)} %bitcast.221), calls=%async_computation.10 | async-start | bytes 8388608
  185.2 52.0 %collective-permute-start.5 = (bf16[3,32,16,3,256]{4,2,3,1,0:T(8,128)(2,1)S(1)}, bf16[3,32,16,3,256]{4,2,3,1,0:T(8,128)(2,1)S(1)}, u32[]{:S(2)}, u32[]{:S(2)}) collective-permute-start(bf16[3,32,16,3,256]{4,2,3,1,0:T(8,128)(2,1)S(1)} %fusion.33), channel_id=1, source_target_pairs={{0,16},{16,0},{1,17},{17,1},{2,18},{18,2},{3,19},{19,3},{4,20},{20... | collective-permute-start | bytes 7077896 | tf_op jit(solution)/shard_map/ppermute | solution.py:47
  186.8 6.7 %copy-start.7 = (bf16[128,16,3,256]{3,1,2,0:T(8,128)(2,1)S(1)}, bf16[128,16,3,256]{3,1,2,0:T(8,128)(2,1)}, u32[]{:S(2)}) copy-start(bf16[128,16,3,256]{3,1,2,0:T(8,128)(2,1)} %all-gather.7.cloned.1.call-done) | copy-start | bytes 9437188
  186.8 7.8 %slice-start.3 = ((s8[6291456]{0:T(1024)(128)(4,1)}), s8[2097152]{0:T(1024)(128)(4,1)S(1)}, s32[]{:S(2)}) async-start(s8[6291456]{0:T(1024)(128)(4,1)} %bitcast.221), calls=%async_computation.11 | async-start | bytes 4194304
  194.6 42.6 %copy-start.14 = (bf16[1,32,16,3,256]{4,2,3,1,0:T(8,128)(2,1)S(1)}, bf16[1,32,16,3,256]{4,2,3,1,0:T(8,128)(2,1)}, u32[]{:S(2)}) copy-start(bf16[1,32,16,3,256]{4,2,3,1,0:T(8,128)(2,1)} %get-tuple-element.61) | copy-start | bytes 2359300
  253.2 5.1 %copy-start.26 = (bf16[256,16,1,256]{3,1,2,0:T(8,128)(2,1)S(1)}, bf16[256,16,1,256]{3,1,2,0:T(8,128)(2,1)}, u32[]{:S(2)}) copy-start(bf16[256,16,1,256]{3,1,2,0:T(8,128)(2,1)} %get-tuple-element.55) | copy-start | bytes 6291460
  258.2 10.3 %copy-start.1 = (bf16[256,4096]{1,0:T(8,128)(2,1)}, bf16[256,4096]{1,0:T(8,128)(2,1)S(1)}, u32[]{:S(2)}) copy-start(bf16[256,4096]{1,0:T(8,128)(2,1)S(1)} %fusion.16) | copy-start | bytes 6291460
  268.6 29.2 %collective-permute-start.6 = (bf16[256,2048]{1,0:T(8,128)(2,1)}, bf16[256,2048]{1,0:T(8,128)(2,1)}, u32[]{:S(2)}, u32[]{:S(2)}) collective-permute-start(bf16[256,2048]{1,0:T(8,128)(2,1)} %bitcast.110), channel_id=1, source_target_pairs={{0,1},{1,0},{2,3},{3,2},{4,5},{5,4},{6,7},{7,6},{8,9},{9,8},{10,11... | collective-permute-start | bytes 3145736 | tf_op jit(solution)/shard_map/ppermute | solution.py:19
  270.9 10.4 %slice-start = ((s8[6291456]{0:T(1024)(128)(4,1)}), s8[2097152]{0:T(1024)(128)(4,1)S(1)}, s32[]{:S(2)}) async-start(s8[6291456]{0:T(1024)(128)(4,1)} %bitcast.210), calls=%async_computation.8 | async-start | bytes 4194304
  275.7 5.0 %copy-start.2 = (bf16[256,4096]{1,0:T(8,128)(2,1)S(1)}, bf16[256,4096]{1,0:T(8,128)(2,1)}, u32[]{:S(2)}) copy-start(bf16[256,4096]{1,0:T(8,128)(2,1)} %copy-done.1) | copy-start | bytes 6291460
  275.7 5.6 %slice-start.1 = ((s8[6291456]{0:T(1024)(128)(4,1)}), s8[4194304]{0:T(1024)(128)(4,1)S(1)}, s32[]{:S(2)}) async-start(s8[6291456]{0:T(1024)(128)(4,1)} %bitcast.210), calls=%async_computation.9 | async-start | bytes 8388608
  279.2 25.9 %collective-permute-start.7 = (bf16[256,2048]{1,0:T(8,128)(2,1)}, bf16[256,2048]{1,0:T(8,128)(2,1)}, u32[]{:S(2)}, u32[]{:S(2)}) collective-permute-start(bf16[256,2048]{1,0:T(8,128)(2,1)} %bitcast.112), channel_id=1, source_target_pairs={{0,2},{2,0},{1,3},{3,1},{4,6},{6,4},{5,7},{7,5},{8,10},{10,8},{9,1... | collective-permute-start | bytes 3145736 | tf_op jit(solution)/shard_map/ppermute | solution.py:19
  297.8 7.5 %copy-start.3 = (bf16[256,4096]{1,0:T(8,128)(2,1)S(1)}, bf16[256,4096]{1,0:T(8,128)(2,1)}, u32[]{:S(2)}) copy-start(bf16[256,4096]{1,0:T(8,128)(2,1)} %copy-done.1) | copy-start | bytes 6291460
  305.1 153.1 %reduce-scatter.8.cloned.1.call-start = ((), (), s32[]{:S(2)}) async-start(), calls=%async_computation.5 | async-start | bytes 1966080 | tf_op jit(solution)/shard_map/reduce_scatter | solution.py:206
  306.1 1.4 collective-permute-start.8
  307.5 5.6 %collective-permute-start.9 = (f32[256,128]{1,0:T(8,128)S(1)}, f32[256,128]{1,0:T(8,128)S(1)}, u32[]{:S(2)}, u32[]{:S(2)}) collective-permute-start(f32[256,128]{1,0:T(8,128)S(1)} %add.97), channel_id=1, source_target_pairs={{0,2},{2,0},{1,3},{3,1},{4,6},{6,4},{5,7},{7,5},{8,10},{10,8},{9,1... | collective-permute-start | bytes 393224 | tf_op jit(solution)/shard_map/ppermute | solution.py:19
  (17 other events, 54.8 us)
Sparse Core Ops, SparseCore 0:
  10.2 66.1 all-gather.4
  77.9 62.0 all-gather.6
  182.6 109.6 reduce-scatter.3
  305.2 109.9 reduce-scatter.5
  422.2 35.9 reduce-scatter.7

commit v2 on v1

--- a/solution.py
+++ b/solution.py
@@ -137,10 +137,7 @@
     ).astype(jnp.bfloat16)
     down_parts, down_fetched = lax.optimization_barrier((down_parts, down_fetched))
     down_full = swap_shares(down_fetched, down_blocks)
-    grad_down = lax.psum_scatter(
-        down_parts, "dp", scatter_dimension=0, tiled=False
-    ).astype(jnp.float32)
-    grad_down = jnp.transpose(grad_down, (1, 0, 2, 3))
+    down_summed = lax.psum_scatter(down_parts, "dp", scatter_dimension=0, tiled=False)
     grad_hidden = jnp.einsum(
         "thso,jhso->thj", picked, down_full, preferred_element_type=jnp.float32
     ).reshape(tokens_here, -1)
@@ -168,21 +165,24 @@
         swapped(section_term(level_bit + 1).astype(jnp.bfloat16), "tensor", level_bit)
         for level_bit in range(section_count - 1)
     ]
-    up_parts, incoming, _ = lax.optimization_barrier(
-        ((up_parts * inv_root).astype(jnp.bfloat16), incoming, grad_down)
+    up_parts, down_summed = lax.optimization_barrier(
+        ((up_parts * inv_root).astype(jnp.bfloat16), down_summed)
+    )
+    grad_down = jnp.transpose(down_summed.astype(jnp.float32), (1, 0, 2, 3))
+    back_part = lax.dot_general(
+        grad_pre, low_right, (((1,), (1,)), ((), ())), preferred_element_type=jnp.float32
+    )
+    back_low = butterfly_sum(back_part, "tensor").astype(jnp.bfloat16)
+    grad_up = lax.psum_scatter(up_parts, "dp", scatter_dimension=0, tiled=False).astype(jnp.float32)
+    row_part, low_row_part, grad_up, incoming = lax.optimization_barrier(
+        (back_low, low_sum, grad_up, incoming)
     )
     own_term = section_term(0)
     for level_bit in range(section_count - 1):
         own_term = own_term + incoming[level_bit].astype(jnp.float32)
-    back_part = lax.dot_general(
-        grad_pre, low_right, (((1,), (1,)), ((), ())), preferred_element_type=jnp.float32
-    )
-    back_low = butterfly_sum(back_part, "tensor").astype(jnp.bfloat16)
     grad_input = (
         own_term + jnp.dot(back_low, low_left, preferred_element_type=jnp.float32)
     ).astype(jnp.bfloat16)
-    grad_up = lax.psum_scatter(up_parts, "dp", scatter_dimension=0, tiled=False).astype(jnp.float32)
-    row_part, low_row_part, grad_up = lax.optimization_barrier((back_low, low_sum, grad_up))
     grad_up = jnp.transpose(grad_up, (2, 0, 1, 3))
     left_parts = jnp.stack(
         split_rows(

time: 471 us -> 461 us (0.979)
  waiting for transfers between devices: 246 us -> 239 us
    reduce_scatter x1, waiting for transfers between devices: 102 us -> 58.5 us  [shards(): lax.psum_scatter(up_parts, 'dp', scatter_dimension=0, tiled=False)]
    reduce_scatter x1, waiting for transfers between devices: 0.01 us -> 18.3 us  [shards(): lax.psum_scatter(down_parts, 'dp', scatter_dimension=0, tiled=False)]
    ppermute x8, waiting for transfers between devices: 16.2 us -> 29 us  [swapped(): return lax.ppermute(block, axis, route)]
    ppermute x2, waiting for transfers between devices: 53 us -> 58 us  [swap_shares(): got = lax.ppermute(send, 'groups', [(0, 1), (1, 0)])]
    unnamed x76 -> x70, local copies, waits for them, and re-layouts: 17.7 us -> 18.5 us
  transfers between devices with their start and end apart: 15 -> 15, of which waited for: 9 -> 9; matrix products, arithmetic and copies ran while one was open for 39% -> 40% of each run, Pallas kernels for 0% -> 0%
where the time goes in v2:
time: 461 us; the launch traced here: 458 us
  waiting for transfers between devices  239 us (52%)
  local copies, waits for them, and re-layouts  80.3 us (17%)
  other arithmetic  57.8 us (13%)
  matrix products  56.4 us (12%)
  between operations  14.6 us (3%)
  starting transfers between devices  10.3 us (2%)
    reduce_scatter x1, waiting for transfers between devices, shards(): lax.psum_scatter(up_parts, 'dp', scatter_dimension=0, tiled=False)  58.5 us
    all_gather x2, waiting for transfers between devices, fetch_share(): return lax.all_gather(mine, 'dp', axis=0, tiled=False)  58.4 us
    ppermute x2, waiting for transfers between devices, swap_shares(): got = lax.ppermute(send, 'groups', [(0, 1), (1, 0)])  58 us
    ppermute x8, waiting for transfers between devices, swapped(): return lax.ppermute(block, axis, route)  29 us
    unnamed x70, local copies, waits for them, and re-layouts  18.5 us
    reduce_scatter x1, waiting for transfers between devices, shards(): lax.psum_scatter(down_parts, 'dp', scatter_dimension=0, tiled=False)  18.3 us
    another operation x5, other arithmetic, pick_blocks(): return jnp.stack(picked, axis=2)  17.7 us
    reduce_scatter x1, waiting for transfers between devices, shards(): lax.psum_scatter(joined, 'dp', scatter_dimension=0, tiled=False)  16.2 us
  transfers between devices with their start and end apart: 15, of which 9 were waited for; matrix products, arithmetic and copies ran while one was open for 40% of the time, Pallas kernels for 0%

profile of v2, /device:TPU:0, one launch (start us, length us, event | category | flops | bytes accessed | tf_op | source)
XLA Modules:
  0.0 458.0 jit_solution(4899865906568123492)
XLA Ops:
  17.9 58.4 %all-gather.5.cloned.1.call-done = bf16[128,16,3,256]{3,1,2,0:T(8,128)(2,1)} async-done(((bf16[32,16,3,256]{3,1,2,0:T(8,128)(2,1)}), bf16[128,16,3,256]{3,1,2,0:T(8,128)(2,1)}) %all-gather.5.cloned.1.call-update) | async-done | bytes 3145744 | tf_op jit(solution)/shard_map/all_gather | solution.py:29
  76.4 4.0 fusion.34
  94.5 4.8 %select_bitcast_fusion = (bf16[256,16,1,256]{3,0,2,1:T(8,128)(2,1)}, bf16[256,16,1,256]{3,0,2,1:T(8,128)(2,1)}) fusion(bf16[16,256,256]{2,1,0:T(8,128)(2,1)} %gather_fusion.5, pred[16]{0:T(512)(128)(4,1)S(1)} %get-tuple-element.74, bf16[16,256,256]{2,1,0:T(8,128)(2,1)} %gather_fusion.4, pred[16]{0:T(512)(128)(4,1)S(1)} %get-tuple-element.76), kind=kLoop, calls=%fused_computation.82 | loop fusion | flops 2097152 | bytes 8388640 | tf_op jit(solution)/shard_map/stack | solution.py:97
  104.8 3.5 collective-permute-done.4
  115.4 4.7 %select_bitcast_fusion.3 = (bf16[256,16,1,256]{3,0,2,1:T(8,128)(2,1)}, bf16[256,16,1,256]{3,0,2,1:T(8,128)(2,1)}) fusion(bf16[16,256,256]{2,1,0:T(8,128)(2,1)} %gather_fusion.2, pred[16]{0:T(512)(128)(4,1)S(1)} %get-tuple-element.78, bf16[16,256,256]{2,1,0:T(8,128)(2,1)} %gather_fusion.1, pred[16]{0:T(512)(128)(4,1)S(1)} %get-tuple-element.80), kind=kLoop, calls=%fused_computation.85 | loop fusion | flops 2097152 | bytes 8388640 | tf_op jit(solution)/shard_map/stack | solution.py:97
  120.1 13.4 %collective-permute-done = bf16[3,32,16,3,256]{4,2,3,1,0:T(8,128)(2,1)} collective-permute-done((bf16[3,32,16,3,256]{4,2,3,1,0:T(8,128)(2,1)}, bf16[3,32,16,3,256]{4,2,3,1,0:T(8,128)(2,1)}, u32[]{:S(2)}, u32[]{:S(2)}) %collective-permute-start) | collective-permute-done | bytes 2359328 | tf_op jit(solution)/shard_map/ppermute | solution.py:47
  133.5 3.5 fusion.23
  137.0 4.4 fusion.7
  141.4 11.1 %fusion.8 = f32[16,256,256,1]{2,1,3,0:T(8,128)} fusion(bf16[256,16,3,256]{3,1,2,0:T(8,128)(2,1)S(1)} %bitcast.218, bf16[256,16,1,256]{3,0,2,1:T(8,128)(2,1)} %get-tuple-element.84, bf16[256,16,1,256]{3,0,2,1:T(8,128)(2,1)} %get-tuple-element.85, bf16[256,16,1,256]{3,0,2,1:T(8,128)(2,1)} %select_bitcast_fusion.5), kind=kOutput, calls=%fused_computation.38 | convolution fusion | flops 1616904192 | bytes 16777216 | tf_op jit(solution)/shard_map/thsi,ihsj->thj/dot_general | solution.py:117
  152.5 5.6 %copy.99 = f32[256,4096]{1,0:T(8,128)} copy(f32[256,4096]{0,1:T(8,128)} %bitcast.231) | data formatting | bytes 8388608 | tf_op jit(solution)/shard_map/reshape | solution.py:122
  158.1 6.6 %multiply_convert_fusion = (bf16[256,4096]{1,0:T(8,128)(2,1)}, f32[256,4096]{1,0:T(8,128)}) fusion(f32[256,4096]{1,0:T(8,128)} %copy.99, bf16[256,128]{1,0:T(8,128)(2,1)S(1)} %add_convert_fusion.2, bf16[128,4096]{1,0:T(8,128)(2,1)S(1)} %copy-done), kind=kOutput, calls=%fused_computation.50 | convolution fusion | flops 278921216 | bytes 11599872 | tf_op jit(solution)/shard_map/dot_general | solution.py:122
  164.7 4.2 copy.152
  178.3 4.1 fusion
  186.7 4.8 %pad_maximum_fusion = bf16[256,16,3,256]{3,0,2,1:T(8,128)(2,1)} fusion(bf16[256,16,1,256]{3,0,2,1:T(8,128)(2,1)S(1)} %copy-done.9, bf16[256,16,1,256]{3,0,2,1:T(8,128)(2,1)S(1)} %copy-done.10, bf16[256,16,1,256]{3,0,2,1:T(8,128)(2,1)} %select_bitcast_fusion.5), kind=kLoop, calls=%fused_computation.30 | loop fusion | flops 6291456 | bytes 12582912 | tf_op jit(solution)/shard_map/stack | solution.py:97
  192.6 44.6 %collective-permute-done.5 = bf16[3,32,16,3,256]{4,2,3,1,0:T(8,128)(2,1)S(1)} collective-permute-done((bf16[3,32,16,3,256]{4,2,3,1,0:T(8,128)(2,1)S(1)}, bf16[3,32,16,3,256]{4,2,3,1,0:T(8,128)(2,1)S(1)}, u32[]{:S(2)}, u32[]{:S(2)}) %collective-permute-start.5) | collective-permute-done | bytes 2359328 | tf_op jit(solution)/shard_map/ppermute | solution.py:47
  240.3 3.6 fusion.4
  244.0 3.4 fusion.67
  247.4 5.8 %copy.143 = f32[256,4096]{1,0:T(8,128)} copy(f32[256,4096]{0,1:T(8,128)} %bitcast.230) | data formatting | bytes 8388608 | tf_op jit(solution)/shard_map/reshape | solution.py:143
  253.2 5.5 %fusion.16 = bf16[256,4096]{1,0:T(8,128)(2,1)S(1)} fusion(f32[256,4096]{1,0:T(8,128)} %copy.143, f32[256,4096]{1,0:T(8,128)} %get-tuple-element.83), kind=kLoop, calls=%fused_computation.49 | loop fusion | flops 19922944 | bytes 10485760 | tf_op jit(solution)/shard_map/convert_element_type | solution.py:144
  269.8 4.0 fusion.1
  273.8 18.3 %reduce-scatter.4.cloned.1.call-done = bf16[1,16,64,3,256]{4,2,3,1,0:T(8,128)(2,1)} async-done(((bf16[4,16,64,3,256]{4,2,3,1,0:T(8,128)(2,1)}), bf16[1,16,64,3,256]{4,2,3,1,0:T(8,128)(2,1)}) %reduce-scatter.4.cloned.1.call-update) | async-done | bytes 1572880 | tf_op jit(solution)/shard_map/reduce_scatter | solution.py:140
  292.3 5.5 %fusion.68 = (bf16[256,16,1,256]{3,1,2,0:T(8,128)(2,1)}, bf16[256,16,1,256]{3,1,2,0:T(8,128)(2,1)S(1)}, bf16[256,16,1,256]{3,1,2,0:T(8,128)(2,1)}) fusion(bf16[256,16,3,256]{3,1,2,0:T(8,128)(2,1)} %bitcast.219), kind=kLoop, calls=%fused_computation.158 | loop fusion | bytes 12582912 | tf_op jit(solution)/shard_map/slice | solution.py:158
  300.1 4.9 %copy.123 = bf16[256,16,256]{2,1,0:T(8,128)(2,1)} copy(bf16[256,16,256]{0,2,1:T(8,128)(2,1)} %convolution_bitcast_fusion.1) | data formatting | bytes 4194304 | tf_op jit(solution)/shard_map/thj,ihj->thi/transpose | solution.py:155
  310.7 4.6 copy.126
  322.8 24.3 %collective-permute-done.7 = f32[256,128]{1,0:T(8,128)S(1)} collective-permute-done((f32[256,128]{1,0:T(8,128)S(1)}, f32[256,128]{1,0:T(8,128)S(1)}, u32[]{:S(2)}, u32[]{:S(2)}) %collective-permute-start.7) | collective-permute-done | bytes 131104 | tf_op jit(solution)/shard_map/ppermute | solution.py:19
  347.2 58.5 %reduce-scatter.6.cloned.1.call-done = bf16[1,16,3,64,256]{4,3,2,1,0:T(8,128)(2,1)} async-done(((bf16[4,16,3,64,256]{4,3,2,1,0:T(8,128)(2,1)}), bf16[1,16,3,64,256]{4,3,2,1,0:T(8,128)(2,1)}) %reduce-scatter.6.cloned.1.call-update) | async-done | bytes 1572880 | tf_op jit(solution)/shard_map/reduce_scatter | solution.py:176
  405.6 3.5 bitcast_convert_fusion
  412.5 3.9 convolution_bitcast_fusion.2
  416.5 3.6 copy.112
  422.4 3.5 copy.128
  425.9 3.5 copy.127
  432.5 16.2 %reduce-scatter.8.cloned.1.call-done = bf16[1,32,6144]{2,1,0:T(8,128)(2,1)} async-done(((bf16[4,32,6144]{2,1,0:T(8,128)(2,1)}), bf16[1,32,6144]{2,1,0:T(8,128)(2,1)}) %reduce-scatter.8.cloned.1.call-update) | async-done | bytes 393232 | tf_op jit(solution)/shard_map/reduce_scatter | solution.py:206
  (152 shorter events, 92.9 us)
Async XLA Ops:
  7.2 150.9 %copy-start = (bf16[128,4096]{1,0:T(8,128)(2,1)S(1)}, bf16[128,4096]{1,0:T(8,128)(2,1)}, u32[]{:S(2)}) copy-start(bf16[128,4096]{1,0:T(8,128)(2,1)} %param.15) | copy-start | bytes 3145732
  7.2 7.2 %copy-start.19 = (bf16[128,2048]{1,0:T(8,128)(2,1)S(1)}, bf16[128,2048]{1,0:T(8,128)(2,1)}, u32[]{:S(2)}) copy-start(bf16[128,2048]{1,0:T(8,128)(2,1)} %param.14) | copy-start | bytes 1572868
  7.2 69.2 %all-gather.5.cloned.1.call-start = ((), (), s32[]{:S(2)}) async-start(), calls=%async_computation.6 | async-start | bytes 3932160 | tf_op jit(solution)/shard_map/all_gather | solution.py:29
  10.1 172.3 %all-gather.7.cloned.1.call-start = ((), (), s32[]{:S(2)}) async-start(), calls=%async_computation.7 | async-start | bytes 3932160 | tf_op jit(solution)/shard_map/all_gather | solution.py:29
  11.4 6.4 %copy-start.28 = (s32[16,3]{0,1:T(4,128)S(1)}, s32[16,3]{0,1:T(4,128)}, u32[]{:S(2)}) copy-start(s32[16,3]{0,1:T(4,128)} %param.17) | copy-start | bytes 580
  11.4 97.0 %collective-permute-start.1 = (bf16[256,2048]{0,1:T(8,128)(2,1)}, bf16[256,2048]{0,1:T(8,128)(2,1)}, u32[]{:S(2)}, u32[]{:S(2)}) collective-permute-start(bf16[256,2048]{0,1:T(8,128)(2,1)} %copy.92), channel_id=1, source_target_pairs={{0,1},{1,0},{2,3},{3,2},{4,5},{5,4},{6,7},{7,6},{8,9},{9,8},{10,11... | collective-permute-start | bytes 3145736 | tf_op jit(solution)/shard_map/ppermute | solution.py:19
  11.9 98.0 %collective-permute-start.2 = (bf16[256,2048]{0,1:T(8,128)(2,1)}, bf16[256,2048]{0,1:T(8,128)(2,1)}, u32[]{:S(2)}, u32[]{:S(2)}) collective-permute-start(bf16[256,2048]{0,1:T(8,128)(2,1)} %copy.92), channel_id=1, source_target_pairs={{0,2},{2,0},{1,3},{3,1},{4,6},{6,4},{5,7},{7,5},{8,10},{10,8},{9,1... | collective-permute-start | bytes 3145736 | tf_op jit(solution)/shard_map/ppermute | solution.py:19
  14.9 88.5 %collective-permute-start.3 = (f32[256,128]{1,0:T(8,128)S(1)}, f32[256,128]{1,0:T(8,128)S(1)}, u32[]{:S(2)}, u32[]{:S(2)}) collective-permute-start(f32[256,128]{1,0:T(8,128)S(1)} %fusion.69), channel_id=1, source_target_pairs={{0,1},{1,0},{2,3},{3,2},{4,5},{5,4},{6,7},{7,6},{8,9},{9,8},{10,11... | collective-permute-start | bytes 393224 | tf_op jit(solution)/shard_map/ppermute | solution.py:19
  17.8 274.4 %reduce-scatter.4.cloned.1.call-start = ((), (), s32[]{:S(2)}) async-start(), calls=%async_computation.3 | async-start | bytes 7864320 | tf_op jit(solution)/shard_map/reduce_scatter | solution.py:140
  76.4 7.2 %copy-start.26 = (bf16[256,2048]{1,0:T(8,128)(2,1)S(1)}, bf16[256,2048]{1,0:T(8,128)(2,1)}, u32[]{:S(2)}) copy-start(bf16[256,2048]{1,0:T(8,128)(2,1)} %param.11) | copy-start | bytes 3145732
  80.4 53.1 %collective-permute-start = (bf16[3,32,16,3,256]{4,2,3,1,0:T(8,128)(2,1)}, bf16[3,32,16,3,256]{4,2,3,1,0:T(8,128)(2,1)}, u32[]{:S(2)}, u32[]{:S(2)}) collective-permute-start(bf16[3,32,16,3,256]{4,2,3,1,0:T(8,128)(2,1)} %fusion.34), channel_id=1, source_target_pairs={{0,16},{16,0},{1,17},{17,1},{2,18},{18,2},{3,19},{19,3},{4,20},{20... | collective-permute-start | bytes 7077896 | tf_op jit(solution)/shard_map/ppermute | solution.py:47
  94.5 4.8 %copy-start.12 = (bf16[16,256,256]{2,1,0:T(8,128)(2,1)S(1)}, bf16[16,256,256]{2,1,0:T(8,128)(2,1)}, u32[]{:S(2)}) copy-start(bf16[16,256,256]{2,1,0:T(8,128)(2,1)} %gather_fusion) | copy-start | bytes 6291460
  103.4 5.0 %collective-permute-start.4 = (f32[256,128]{1,0:T(8,128)S(1)}, f32[256,128]{1,0:T(8,128)S(1)}, u32[]{:S(2)}, u32[]{:S(2)}) collective-permute-start(f32[256,128]{1,0:T(8,128)S(1)} %add.88), channel_id=1, source_target_pairs={{0,2},{2,0},{1,3},{3,1},{4,6},{6,4},{5,7},{7,5},{8,10},{10,8},{9,1... | collective-permute-start | bytes 393224 | tf_op jit(solution)/shard_map/ppermute | solution.py:19
  115.3 18.2 %copy-start.14 = (bf16[1,32,16,3,256]{4,2,3,1,0:T(8,128)(2,1)S(1)}, bf16[1,32,16,3,256]{4,2,3,1,0:T(8,128)(2,1)}, u32[]{:S(2)}) copy-start(bf16[1,32,16,3,256]{4,2,3,1,0:T(8,128)(2,1)} %get-tuple-element.65) | copy-start | bytes 2359300
  141.4 11.1 %copy-start.3 = (bf16[4,2,32,16,3,256]{5,3,4,2,1,0:T(8,128)(2,1)}, bf16[4,2,32,16,3,256]{5,3,4,2,1,0:T(8,128)(2,1)S(1)}, u32[]{:S(2)}) copy-start(bf16[4,2,32,16,3,256]{5,3,4,2,1,0:T(8,128)(2,1)S(1)} %fusion.7) | copy-start | bytes 18874372
  164.7 4.2 copy-start.15
  169.0 4.3 copy-start.23
  182.4 4.3 copy-start.9
  182.4 223.2 %reduce-scatter.6.cloned.1.call-start = ((), (), s32[]{:S(2)}) async-start(), calls=%async_computation.4 | async-start | bytes 7864320 | tf_op jit(solution)/shard_map/reduce_scatter | solution.py:176
  182.4 4.2 copy-start.10
  185.1 6.4 %copy-start.5 = (bf16[128,16,3,256]{3,1,2,0:T(8,128)(2,1)S(1)}, bf16[128,16,3,256]{3,1,2,0:T(8,128)(2,1)}, u32[]{:S(2)}) copy-start(bf16[128,16,3,256]{3,1,2,0:T(8,128)(2,1)} %all-gather.7.cloned.1.call-done) | copy-start | bytes 9437188
  185.1 52.0 %collective-permute-start.5 = (bf16[3,32,16,3,256]{4,2,3,1,0:T(8,128)(2,1)S(1)}, bf16[3,32,16,3,256]{4,2,3,1,0:T(8,128)(2,1)S(1)}, u32[]{:S(2)}, u32[]{:S(2)}) collective-permute-start(bf16[3,32,16,3,256]{4,2,3,1,0:T(8,128)(2,1)S(1)} %fusion.33), channel_id=1, source_target_pairs={{0,16},{16,0},{1,17},{17,1},{2,18},{18,2},{3,19},{19,3},{4,20},{20... | collective-permute-start | bytes 7077896 | tf_op jit(solution)/shard_map/ppermute | solution.py:47
  191.5 45.7 %copy-start.13 = (bf16[1,32,16,3,256]{4,2,3,1,0:T(8,128)(2,1)S(1)}, bf16[1,32,16,3,256]{4,2,3,1,0:T(8,128)(2,1)}, u32[]{:S(2)}) copy-start(bf16[1,32,16,3,256]{4,2,3,1,0:T(8,128)(2,1)} %get-tuple-element.63) | copy-start | bytes 2359300
  240.3 3.7 copy-start.16
  247.4 13.3 %slice-start = ((s8[6291456]{0:T(1024)(128)(4,1)}), s8[2097152]{0:T(1024)(128)(4,1)S(1)}, s32[]{:S(2)}) async-start(s8[6291456]{0:T(1024)(128)(4,1)} %bitcast.208), calls=%async_computation.8 | async-start | bytes 4194304
  253.2 7.6 %slice-start.1 = ((s8[6291456]{0:T(1024)(128)(4,1)}), s8[4194304]{0:T(1024)(128)(4,1)S(1)}, s32[]{:S(2)}) async-start(s8[6291456]{0:T(1024)(128)(4,1)} %bitcast.208), calls=%async_computation.9 | async-start | bytes 8388608
  292.2 156.4 %reduce-scatter.8.cloned.1.call-start = ((), (), s32[]{:S(2)}) async-start(), calls=%async_computation.5 | async-start | bytes 1966080 | tf_op jit(solution)/shard_map/reduce_scatter | solution.py:206
  292.3 5.5 %copy-start.2 = (bf16[256,4096]{1,0:T(8,128)(2,1)S(1)}, bf16[256,4096]{1,0:T(8,128)(2,1)}, u32[]{:S(2)}) copy-start(bf16[256,4096]{1,0:T(8,128)(2,1)} %copy-done.1) | copy-start | bytes 6291460
  308.4 100.7 %collective-permute-start.8 = (bf16[256,2048]{1,0:T(8,128)(2,1)}, bf16[256,2048]{1,0:T(8,128)(2,1)}, u32[]{:S(2)}, u32[]{:S(2)}) collective-permute-start(bf16[256,2048]{1,0:T(8,128)(2,1)} %bitcast.109), channel_id=1, source_target_pairs={{0,1},{1,0},{2,3},{3,2},{4,5},{5,4},{6,7},{7,6},{8,9},{9,8},{10,11... | collective-permute-start | bytes 3145736 | tf_op jit(solution)/shard_map/ppermute | solution.py:19
  318.6 90.5 %collective-permute-start.9 = (bf16[256,2048]{1,0:T(8,128)(2,1)}, bf16[256,2048]{1,0:T(8,128)(2,1)}, u32[]{:S(2)}, u32[]{:S(2)}) collective-permute-start(bf16[256,2048]{1,0:T(8,128)(2,1)} %bitcast.111), channel_id=1, source_target_pairs={{0,2},{2,0},{1,3},{3,1},{4,6},{6,4},{5,7},{7,5},{8,10},{10,8},{9,1... | collective-permute-start | bytes 3145736 | tf_op jit(solution)/shard_map/ppermute | solution.py:19
  320.7 1.4 collective-permute-start.6
  322.2 25.0 %collective-permute-start.7 = (f32[256,128]{1,0:T(8,128)S(1)}, f32[256,128]{1,0:T(8,128)S(1)}, u32[]{:S(2)}, u32[]{:S(2)}) collective-permute-start(f32[256,128]{1,0:T(8,128)S(1)} %add.95), channel_id=1, source_target_pairs={{0,2},{2,0},{1,3},{3,1},{4,6},{6,4},{5,7},{7,5},{8,10},{10,8},{9,1... | collective-permute-start | bytes 393224 | tf_op jit(solution)/shard_map/ppermute | solution.py:19
  (14 other events, 39.5 us)
Sparse Core Ops, SparseCore 0:
  10.2 66.1 all-gather.4
  77.9 62.0 all-gather.6
  182.5 109.6 reduce-scatter.3
  294.3 111.2 reduce-scatter.5
  412.7 35.9 reduce-scatter.7

commit v3 on v2

--- a/solution.py
+++ b/solution.py
@@ -114,23 +114,23 @@
         swapped(inputs, "tensor", level_bit) for level_bit in range(section_count - 1)
     ]
     selected = pick_blocks(sources, up_pattern, block_size)
-    sparse = jnp.einsum("thsi,ihsj->thj", selected, up_full, preferred_element_type=jnp.float32)
+    sparse = jnp.einsum("thsi,ihsj->htj", selected, up_full, preferred_element_type=jnp.float32)
+    right_blocks = low_right.reshape(low_right.shape[0], hidden_here, block_size)
     low_part = lax.dot_general(
         inputs, low_left, (((1,), (1,)), ((), ())), preferred_element_type=jnp.float32
     )
     low_sum = butterfly_sum(low_part, "tensor").astype(jnp.bfloat16)
-    preact = sparse.reshape(tokens_here, -1) + jnp.dot(
-        low_sum, low_right, preferred_element_type=jnp.float32
+    preact = sparse + jnp.einsum(
+        "tr,rhj->htj", low_sum, right_blocks, preferred_element_type=jnp.float32
     )
     activated, slopes = gelu_pair(preact)
     hidden = activated.astype(jnp.bfloat16)
     picked = pick_blocks([cotangent] * section_count, down_pattern, block_size)
-    hidden_blocks = hidden.reshape(tokens_here, hidden_here, block_size)
     down_parts = (
         jnp.stack(
             [
-                jnp.einsum("thj,thso->hjso", rows, picked, preferred_element_type=jnp.float32)
-                for rows in split_rows(hidden_blocks, 2, dp_size)
+                jnp.einsum("htj,thso->hjso", rows, picked, preferred_element_type=jnp.float32)
+                for rows in split_rows(hidden, 2, dp_size)
             ]
         )
         * inv_root
@@ -139,13 +139,12 @@
     down_full = swap_shares(down_fetched, down_blocks)
     down_summed = lax.psum_scatter(down_parts, "dp", scatter_dimension=0, tiled=False)
     grad_hidden = jnp.einsum(
-        "thso,jhso->thj", picked, down_full, preferred_element_type=jnp.float32
-    ).reshape(tokens_here, -1)
-    grad_pre = (grad_hidden * slopes).astype(jnp.bfloat16)
-    grad_blocks = grad_pre.reshape(tokens_here, hidden_here, block_size)
+        "thso,jhso->htj", picked, down_full, preferred_element_type=jnp.float32
+    )
+    grad_blocks = (grad_hidden * slopes).astype(jnp.bfloat16)
     up_parts = jnp.stack(
         [
-            jnp.einsum("thsi,thj->hsij", rows, grad_blocks, preferred_element_type=jnp.float32)
+            jnp.einsum("thsi,htj->hsij", rows, grad_blocks, preferred_element_type=jnp.float32)
             for rows in split_rows(selected, 3, dp_size)
         ]
     )
@@ -153,7 +152,7 @@
 
     def section_term(which_section):
         spread = jnp.einsum(
-            "thj,ihj->thi",
+            "htj,ihj->thi",
             grad_blocks,
             up_full[:, :, which_section, :],
             preferred_element_type=jnp.float32,
@@ -169,8 +168,8 @@
         ((up_parts * inv_root).astype(jnp.bfloat16), down_summed)
     )
     grad_down = jnp.transpose(down_summed.astype(jnp.float32), (1, 0, 2, 3))
-    back_part = lax.dot_general(
-        grad_pre, low_right, (((1,), (1,)), ((), ())), preferred_element_type=jnp.float32
+    back_part = jnp.einsum(
+        "htj,rhj->tr", grad_blocks, right_blocks, preferred_element_type=jnp.float32
     )
     back_low = butterfly_sum(back_part, "tensor").astype(jnp.bfloat16)
     grad_up = lax.psum_scatter(up_parts, "dp", scatter_dimension=0, tiled=False).astype(jnp.float32)
@@ -195,9 +194,9 @@
     )
     right_parts = jnp.stack(
         split_rows(
-            lax.dot_general(
-                low_row_part, grad_pre, (((0,), (0,)), ((), ())), preferred_element_type=jnp.float32
-            ),
+            jnp.einsum(
+                "tr,htj->rhj", low_row_part, grad_blocks, preferred_element_type=jnp.float32
+            ).reshape(low_row_part.shape[1], -1),
             0,
             dp_size,
         )

time: 461 us -> 465 us (level)
  waiting for transfers between devices: 239 us -> 251 us
  other arithmetic: 57.8 us -> 52 us
    reshape x3 -> x0, local copies, waits for them, and re-layouts: 15.6 us -> none  [the longest x1 5.78 us: shards(): grad_hidden = jnp.einsum('thso,jhso->thj', picked, down_full, preferred_e...]
    reduce_scatter x1, waiting for transfers between devices: 18.3 us -> 30.7 us  [shards(): lax.psum_scatter(down_parts, 'dp', scatter_dimension=0, tiled=False)]
    slice x0 -> x5, local copies, waits for them, and re-layouts: none -> 8.74 us  [split_rows(): lax.slice_in_dim(values, d * rows, (d + 1) * rows, axis=axis)]
    another operation x1 -> x4, local copies, waits for them, and re-layouts: 0.19 us -> 6.93 us  [shards(): jnp.stack(split_rows(jnp.einsum('tr,htj->rhj', low_row_part, grad_blocks,...]
    convert_element_type x2 -> x1, other arithmetic: 9.59 us -> 4.07 us  [shards(): down_parts = (jnp.stack([jnp.einsum('htj,thso->hjso', rows, picked, prefe...]
    unnamed x70 -> x63, local copies, waits for them, and re-layouts: 18.5 us -> 14.4 us
  transfers between devices with their start and end apart: 15 -> 15, of which waited for: 9 -> 9; matrix products, arithmetic and copies ran while one was open for 40% -> 34% of each run, Pallas kernels for 0% -> 0%
where the time goes in v3:
time: 465 us; the launch traced here: 461 us
  waiting for transfers between devices  251 us (54%)
  local copies, waits for them, and re-layouts  75.7 us (16%)
  matrix products  57.2 us (12%)
  other arithmetic  52 us (11%)
  between operations  14.5 us (3%)
  starting transfers between devices  10.6 us (2%)
    reduce_scatter x1, waiting for transfers between devices, shards(): lax.psum_scatter(up_parts, 'dp', scatter_dimension=0, tiled=False)  58.7 us
    ppermute x2, waiting for transfers between devices, swap_shares(): got = lax.ppermute(send, 'groups', [(0, 1), (1, 0)])  58.5 us
    all_gather x2, waiting for transfers between devices, fetch_share(): return lax.all_gather(mine, 'dp', axis=0, tiled=False)  58 us
    reduce_scatter x1, waiting for transfers between devices, shards(): lax.psum_scatter(down_parts, 'dp', scatter_dimension=0, tiled=False)  30.7 us
    ppermute x8, waiting for transfers between devices, swapped(): return lax.ppermute(block, axis, route)  29 us
    reduce_scatter x1, waiting for transfers between devices, shards(): lax.psum_scatter(joined, 'dp', scatter_dimension=0, tiled=False)  16.3 us
    another operation x5, other arithmetic, pick_blocks(): return jnp.stack(picked, axis=2)  16.1 us
    unnamed x63, local copies, waits for them, and re-layouts  14.4 us
  transfers between devices with their start and end apart: 15, of which 9 were waited for; matrix products, arithmetic and copies ran while one was open for 34% of the time, Pallas kernels for 0%

profile of v3, /device:TPU:0, one launch (start us, length us, event | category | flops | bytes accessed | tf_op | source)
XLA Modules:
  0.0 461.3 jit_solution(16585081722519907757)
XLA Ops:
  7.2 2.7 dynamic-slice_bitcast_fusion.1
  11.4 3.0 collective-permute-start.2
  18.4 58.0 %all-gather.5.cloned.1.call-done = bf16[128,16,3,256]{3,1,2,0:T(8,128)(2,1)} async-done(((bf16[32,16,3,256]{3,1,2,0:T(8,128)(2,1)}), bf16[128,16,3,256]{3,1,2,0:T(8,128)(2,1)}) %all-gather.5.cloned.1.call-update) | async-done | bytes 3145744 | tf_op jit(solution)/shard_map/all_gather | solution.py:29
  76.3 4.0 fusion.34
  94.4 4.9 %select_bitcast_fusion.3 = (bf16[256,16,1,256]{3,0,2,1:T(8,128)(2,1)}, bf16[256,16,1,256]{3,0,2,1:T(8,128)(2,1)}) fusion(bf16[16,256,256]{2,1,0:T(8,128)(2,1)} %gather_fusion.2, pred[16]{0:T(512)(128)(4,1)S(1)} %copy-done.24, bf16[16,256,256]{2,1,0:T(8,128)(2,1)} %gather_fusion.1, pred[16]{0:T(512)(128)(4,1)S(1)} %copy-done.25), kind=kLoop, calls=%fused_computation.86 | loop fusion | flops 2097152 | bytes 8388640 | tf_op jit(solution)/shard_map/stack | solution.py:97
  105.8 3.5 collective-permute-done.4
  116.4 4.8 %select_bitcast_fusion = (bf16[256,16,1,256]{3,0,2,1:T(8,128)(2,1)}, bf16[256,16,1,256]{3,0,2,1:T(8,128)(2,1)}) fusion(bf16[16,256,256]{2,1,0:T(8,128)(2,1)} %gather_fusion.5, pred[16]{0:T(512)(128)(4,1)S(1)} %get-tuple-element.78, bf16[16,256,256]{2,1,0:T(8,128)(2,1)} %gather_fusion.4, pred[16]{0:T(512)(128)(4,1)S(1)} %get-tuple-element.80), kind=kLoop, calls=%fused_computation.83 | loop fusion | flops 2097152 | bytes 8388640 | tf_op jit(solution)/shard_map/stack | solution.py:97
  121.2 12.3 %collective-permute-done = bf16[3,32,16,3,256]{4,2,3,1,0:T(8,128)(2,1)} collective-permute-done((bf16[3,32,16,3,256]{4,2,3,1,0:T(8,128)(2,1)}, bf16[3,32,16,3,256]{4,2,3,1,0:T(8,128)(2,1)}, u32[]{:S(2)}, u32[]{:S(2)}) %collective-permute-start) | collective-permute-done | bytes 2359328 | tf_op jit(solution)/shard_map/ppermute | solution.py:47
  133.5 3.5 fusion.23
  137.0 4.4 fusion.7
  141.4 11.0 %fusion.8 = f32[16,256,256,1]{1,2,3,0:T(8,128)} fusion(bf16[256,16,3,256]{3,1,2,0:T(8,128)(2,1)S(1)} %bitcast.218, bf16[256,16,1,256]{3,0,2,1:T(8,128)(2,1)} %get-tuple-element.84, bf16[256,16,1,256]{3,0,2,1:T(8,128)(2,1)} %get-tuple-element.85, bf16[256,16,1,256]{3,0,2,1:T(8,128)(2,1)} %select_bitcast_fusion.2), kind=kOutput, calls=%fused_computation.38 | convolution fusion | flops 1616904192 | bytes 16777216 | tf_op jit(solution)/shard_map/thsi,ihsj->htj/dot_general | solution.py:117
  152.5 6.5 %multiply_convert_fusion = (bf16[16,256,256]{1,2,0:T(8,128)(2,1)S(1)}, f32[16,256,256]{1,2,0:T(8,128)}) fusion(bf16[16,16,8,256]{3,2,1,0:T(8,128)(2,1)} %bitcast.234, bf16[256,128]{1,0:T(8,128)(2,1)S(1)} %add_convert_fusion.2, f32[16,256,256,1]{1,2,3,0:T(8,128)} %fusion.8), kind=kOutput, calls=%fused_computation.50 | convolution fusion | flops 278921216 | bytes 11599872 | tf_op jit(solution)/shard_map/tr,rhj->htj/dot_general | solution.py:123
  165.4 4.1 fusion
  169.5 2.7 fusion.33
  173.8 3.1 pad_maximum_fusion.1
  178.0 46.3 %collective-permute-done.5 = bf16[3,32,16,3,256]{4,2,3,1,0:T(8,128)(2,1)S(1)} collective-permute-done((bf16[3,32,16,3,256]{4,2,3,1,0:T(8,128)(2,1)S(1)}, bf16[3,32,16,3,256]{4,2,3,1,0:T(8,128)(2,1)S(1)}, u32[]{:S(2)}, u32[]{:S(2)}) %collective-permute-start.5) | collective-permute-done | bytes 2359328 | tf_op jit(solution)/shard_map/ppermute | solution.py:47
  227.4 3.6 fusion.4
  231.1 6.3 %fusion.16 = bf16[16,256,256]{1,2,0:T(8,128)(2,1)S(1)} fusion(f32[16,256,256]{1,2,0:T(8,128)} %get-tuple-element.83, bf16[256,16,3,256]{3,0,2,1:T(8,128)(2,1)S(1)} %bitcast.229, bf16[256,16,1,256]{3,0,2,1:T(8,128)(2,1)S(1)} %copy-done.13, bf16[256,16,1,256]{3,0,2,1:T(8,128)(2,1)S(1)} %copy-done.15, bf16[256,16,1,256]{3,0,2,1:T(8,128)(2,1)S(1)} %copy-done.20), kind=kOutput, calls=%fused_computation.48 | convolution fusion | flops 1636827136 | bytes 18874368 | tf_op jit(solution)/shard_map/thso,jhso->htj/dot_general | solution.py:141
  244.7 3.9 fusion.1
  248.6 30.7 %reduce-scatter.4.cloned.1.call-done = bf16[1,16,64,3,256]{4,2,3,1,0:T(8,128)(2,1)} async-done(((bf16[4,16,64,3,256]{4,2,3,1,0:T(8,128)(2,1)}), bf16[1,16,64,3,256]{4,2,3,1,0:T(8,128)(2,1)}) %reduce-scatter.4.cloned.1.call-update) | async-done | bytes 1572880 | tf_op jit(solution)/shard_map/reduce_scatter | solution.py:140
  279.3 5.3 %fusion.76 = (bf16[256,16,1,256]{3,1,2,0:T(8,128)(2,1)}, bf16[256,16,1,256]{3,1,2,0:T(8,128)(2,1)S(1)}, bf16[256,16,1,256]{3,1,2,0:T(8,128)(2,1)}) fusion(bf16[256,16,3,256]{3,1,2,0:T(8,128)(2,1)} %bitcast.219), kind=kLoop, calls=%fused_computation.155 | loop fusion | bytes 12582912 | tf_op jit(solution)/shard_map/slice | solution.py:157
  286.9 4.9 %copy.129 = bf16[256,16,256]{2,1,0:T(8,128)(2,1)} copy(bf16[256,16,256]{0,2,1:T(8,128)(2,1)} %convolution_bitcast_fusion.1) | data formatting | bytes 4194304 | tf_op jit(solution)/shard_map/htj,ihj->thi/transpose | solution.py:154
  297.4 4.6 copy.132
  309.7 24.3 %collective-permute-done.7 = f32[256,128]{1,0:T(8,128)S(1)} collective-permute-done((f32[256,128]{1,0:T(8,128)S(1)}, f32[256,128]{1,0:T(8,128)S(1)}, u32[]{:S(2)}, u32[]{:S(2)}) %collective-permute-start.7) | collective-permute-done | bytes 131104 | tf_op jit(solution)/shard_map/ppermute | solution.py:19
  334.0 58.7 %reduce-scatter.6.cloned.1.call-done = bf16[1,16,3,64,256]{4,3,2,1,0:T(8,128)(2,1)} async-done(((bf16[4,16,3,64,256]{4,3,2,1,0:T(8,128)(2,1)}), bf16[1,16,3,64,256]{4,3,2,1,0:T(8,128)(2,1)}) %reduce-scatter.6.cloned.1.call-update) | async-done | bytes 1572880 | tf_op jit(solution)/shard_map/reduce_scatter | solution.py:175
  392.7 3.5 bitcast_convert_fusion
  415.8 3.8 convolution_bitcast_fusion.2
  419.6 3.6 copy.116
  425.5 3.5 copy.140
  429.0 3.5 copy.139
  432.5 3.1 add_convert_fusion
  435.6 16.3 %reduce-scatter.8.cloned.1.call-done = bf16[1,32,6144]{2,1,0:T(8,128)(2,1)} async-done(((bf16[4,32,6144]{2,1,0:T(8,128)(2,1)}), bf16[1,32,6144]{2,1,0:T(8,128)(2,1)}) %reduce-scatter.8.cloned.1.call-update) | async-done | bytes 393232 | tf_op jit(solution)/shard_map/reduce_scatter | solution.py:205
  (148 shorter events, 92.5 us)
Async XLA Ops:
  7.2 7.2 %copy-start = (bf16[128,2048]{1,0:T(8,128)(2,1)S(1)}, bf16[128,2048]{1,0:T(8,128)(2,1)}, u32[]{:S(2)}) copy-start(bf16[128,2048]{1,0:T(8,128)(2,1)} %param.14) | copy-start | bytes 1572868
  7.2 69.2 %all-gather.5.cloned.1.call-start = ((), (), s32[]{:S(2)}) async-start(), calls=%async_computation.6 | async-start | bytes 3932160 | tf_op jit(solution)/shard_map/all_gather | solution.py:29
  10.0 159.5 %all-gather.7.cloned.1.call-start = ((), (), s32[]{:S(2)}) async-start(), calls=%async_computation.7 | async-start | bytes 3932160 | tf_op jit(solution)/shard_map/all_gather | solution.py:29
  11.4 6.5 %copy-start.26 = (s32[16,3]{0,1:T(4,128)S(1)}, s32[16,3]{0,1:T(4,128)}, u32[]{:S(2)}) copy-start(s32[16,3]{0,1:T(4,128)} %param.17) | copy-start | bytes 580
  11.4 98.0 %collective-permute-start.2 = (bf16[256,2048]{0,1:T(8,128)(2,1)}, bf16[256,2048]{0,1:T(8,128)(2,1)}, u32[]{:S(2)}, u32[]{:S(2)}) collective-permute-start(bf16[256,2048]{0,1:T(8,128)(2,1)} %copy.104), channel_id=1, source_target_pairs={{0,2},{2,0},{1,3},{3,1},{4,6},{6,4},{5,7},{7,5},{8,10},{10,8},{9,1... | collective-permute-start | bytes 3145736 | tf_op jit(solution)/shard_map/ppermute | solution.py:19
  14.3 96.5 %collective-permute-start.1 = (bf16[256,2048]{0,1:T(8,128)(2,1)}, bf16[256,2048]{0,1:T(8,128)(2,1)}, u32[]{:S(2)}, u32[]{:S(2)}) collective-permute-start(bf16[256,2048]{0,1:T(8,128)(2,1)} %copy.104), channel_id=1, source_target_pairs={{0,1},{1,0},{2,3},{3,2},{4,5},{5,4},{6,7},{7,6},{8,9},{9,8},{10,11... | collective-permute-start | bytes 3145736 | tf_op jit(solution)/shard_map/ppermute | solution.py:19
  14.8 88.6 %collective-permute-start.3 = (f32[256,128]{1,0:T(8,128)S(1)}, f32[256,128]{1,0:T(8,128)}, u32[]{:S(2)}, u32[]{:S(2)}) collective-permute-start(f32[256,128]{1,0:T(8,128)S(1)} %fusion.78), channel_id=1, source_target_pairs={{0,1},{1,0},{2,3},{3,2},{4,5},{5,4},{6,7},{7,6},{8,9},{9,8},{10,11... | collective-permute-start | bytes 393224 | tf_op jit(solution)/shard_map/ppermute | solution.py:19
  17.8 261.5 %reduce-scatter.4.cloned.1.call-start = ((), (), s32[]{:S(2)}) async-start(), calls=%async_computation.3 | async-start | bytes 7864320 | tf_op jit(solution)/shard_map/reduce_scatter | solution.py:140
  76.3 7.2 %copy-start.22 = (bf16[256,2048]{1,0:T(8,128)(2,1)S(1)}, bf16[256,2048]{1,0:T(8,128)(2,1)}, u32[]{:S(2)}) copy-start(bf16[256,2048]{1,0:T(8,128)(2,1)} %param.11) | copy-start | bytes 3145732
  80.3 53.1 %collective-permute-start = (bf16[3,32,16,3,256]{4,2,3,1,0:T(8,128)(2,1)}, bf16[3,32,16,3,256]{4,2,3,1,0:T(8,128)(2,1)}, u32[]{:S(2)}, u32[]{:S(2)}) collective-permute-start(bf16[3,32,16,3,256]{4,2,3,1,0:T(8,128)(2,1)} %fusion.34), channel_id=1, source_target_pairs={{0,16},{16,0},{1,17},{17,1},{2,18},{18,2},{3,19},{19,3},{4,20},{20... | collective-permute-start | bytes 7077896 | tf_op jit(solution)/shard_map/ppermute | solution.py:47
  94.4 4.9 %copy-start.10 = (bf16[16,256,256]{2,1,0:T(8,128)(2,1)S(1)}, bf16[16,256,256]{2,1,0:T(8,128)(2,1)}, u32[]{:S(2)}) copy-start(bf16[16,256,256]{2,1,0:T(8,128)(2,1)} %gather_fusion.3) | copy-start | bytes 6291460
  104.3 5.0 %collective-permute-start.4 = (f32[256,128]{1,0:T(8,128)S(1)}, f32[256,128]{1,0:T(8,128)S(1)}, u32[]{:S(2)}, u32[]{:S(2)}) collective-permute-start(f32[256,128]{1,0:T(8,128)S(1)} %add.88), channel_id=1, source_target_pairs={{0,2},{2,0},{1,3},{3,1},{4,6},{6,4},{5,7},{7,5},{8,10},{10,8},{9,1... | collective-permute-start | bytes 393224 | tf_op jit(solution)/shard_map/ppermute | solution.py:19
  116.4 17.1 %copy-start.11 = (bf16[1,32,16,3,256]{4,2,3,1,0:T(8,128)(2,1)S(1)}, bf16[1,32,16,3,256]{4,2,3,1,0:T(8,128)(2,1)}, u32[]{:S(2)}) copy-start(bf16[1,32,16,3,256]{4,2,3,1,0:T(8,128)(2,1)} %get-tuple-element.65) | copy-start | bytes 2359300
  141.4 11.1 %copy-start.1 = (bf16[4,2,32,16,3,256]{5,3,4,2,1,0:T(8,128)(2,1)}, bf16[4,2,32,16,3,256]{5,3,4,2,1,0:T(8,128)(2,1)S(1)}, u32[]{:S(2)}) copy-start(bf16[4,2,32,16,3,256]{5,3,4,2,1,0:T(8,128)(2,1)S(1)} %fusion.7) | copy-start | bytes 18874372
  152.4 6.5 %copy-start.12 = (bf16[256,16,1,256]{3,0,2,1:T(8,128)(2,1)S(1)}, bf16[256,16,1,256]{3,0,2,1:T(8,128)(2,1)}, u32[]{:S(2)}) copy-start(bf16[256,16,1,256]{3,0,2,1:T(8,128)(2,1)} %get-tuple-element.86) | copy-start | bytes 6291460
  152.4 6.5 %copy-start.14 = (bf16[256,16,1,256]{3,0,2,1:T(8,128)(2,1)S(1)}, bf16[256,16,1,256]{3,0,2,1:T(8,128)(2,1)}, u32[]{:S(2)}) copy-start(bf16[256,16,1,256]{3,0,2,1:T(8,128)(2,1)} %get-tuple-element.87) | copy-start | bytes 6291460
  152.4 6.5 %copy-start.19 = (bf16[256,16,1,256]{3,0,2,1:T(8,128)(2,1)S(1)}, bf16[256,16,1,256]{3,0,2,1:T(8,128)(2,1)}, u32[]{:S(2)}) copy-start(bf16[256,16,1,256]{3,0,2,1:T(8,128)(2,1)} %select_bitcast_fusion.5) | copy-start | bytes 6291460
  169.5 4.3 copy-start.6
  169.5 223.2 %reduce-scatter.6.cloned.1.call-start = ((), (), s32[]{:S(2)}) async-start(), calls=%async_computation.4 | async-start | bytes 7864320 | tf_op jit(solution)/shard_map/reduce_scatter | solution.py:175
  169.5 4.2 copy-start.7
  172.2 4.7 %copy-start.3 = (bf16[128,16,3,256]{3,1,2,0:T(8,128)(2,1)S(1)}, bf16[128,16,3,256]{3,1,2,0:T(8,128)(2,1)}, u32[]{:S(2)}) copy-start(bf16[128,16,3,256]{3,1,2,0:T(8,128)(2,1)} %all-gather.7.cloned.1.call-done) | copy-start | bytes 9437188
  172.2 52.0 %collective-permute-start.5 = (bf16[3,32,16,3,256]{4,2,3,1,0:T(8,128)(2,1)S(1)}, bf16[3,32,16,3,256]{4,2,3,1,0:T(8,128)(2,1)S(1)}, u32[]{:S(2)}, u32[]{:S(2)}) collective-permute-start(bf16[3,32,16,3,256]{4,2,3,1,0:T(8,128)(2,1)S(1)} %fusion.33), channel_id=1, source_target_pairs={{0,16},{16,0},{1,17},{17,1},{2,18},{18,2},{3,19},{19,3},{4,20},{20... | collective-permute-start | bytes 7077896 | tf_op jit(solution)/shard_map/ppermute | solution.py:47
  227.4 3.7 copy-start.13
  227.4 3.7 copy-start.15
  227.4 3.7 copy-start.20
  279.3 172.6 %reduce-scatter.8.cloned.1.call-start = ((), (), s32[]{:S(2)}) async-start(), calls=%async_computation.5 | async-start | bytes 1966080 | tf_op jit(solution)/shard_map/reduce_scatter | solution.py:205
  295.2 101.0 %collective-permute-start.8 = (bf16[256,2048]{1,0:T(8,128)(2,1)}, bf16[256,2048]{1,0:T(8,128)(2,1)}, u32[]{:S(2)}, u32[]{:S(2)}) collective-permute-start(bf16[256,2048]{1,0:T(8,128)(2,1)} %bitcast.99), channel_id=1, source_target_pairs={{0,1},{1,0},{2,3},{3,2},{4,5},{5,4},{6,7},{7,6},{8,9},{9,8},{10,11... | collective-permute-start | bytes 3145736 | tf_op jit(solution)/shard_map/ppermute | solution.py:19
  302.0 4.8 %copy-start.27 = (bf16[128,4096]{1,0:T(8,128)(2,1)S(1)}, bf16[128,4096]{1,0:T(8,128)(2,1)}, u32[]{:S(2)}) copy-start(bf16[128,4096]{1,0:T(8,128)(2,1)} %param.15) | copy-start | bytes 3145732
  305.4 90.8 %collective-permute-start.9 = (bf16[256,2048]{1,0:T(8,128)(2,1)}, bf16[256,2048]{1,0:T(8,128)(2,1)}, u32[]{:S(2)}, u32[]{:S(2)}) collective-permute-start(bf16[256,2048]{1,0:T(8,128)(2,1)} %bitcast.101), channel_id=1, source_target_pairs={{0,2},{2,0},{1,3},{3,1},{4,6},{6,4},{5,7},{7,5},{8,10},{10,8},{9,1... | collective-permute-start | bytes 3145736 | tf_op jit(solution)/shard_map/ppermute | solution.py:19
  307.6 1.4 collective-permute-start.6
  309.0 25.0 %collective-permute-start.7 = (f32[256,128]{1,0:T(8,128)S(1)}, f32[256,128]{1,0:T(8,128)S(1)}, u32[]{:S(2)}, u32[]{:S(2)}) collective-permute-start(f32[256,128]{1,0:T(8,128)S(1)} %add.95), channel_id=1, source_target_pairs={{0,2},{2,0},{1,3},{3,1},{4,6},{6,4},{5,7},{7,5},{8,10},{10,8},{9,1... | collective-permute-start | bytes 393224 | tf_op jit(solution)/shard_map/ppermute | solution.py:19
  425.5 3.5 copy-start.2
  (11 other events, 25.0 us)
Sparse Core Ops, SparseCore 0:
  10.1 66.1 all-gather.4
  77.9 62.0 all-gather.6
  169.6 109.6 reduce-scatter.3
  281.4 111.2 reduce-scatter.5
  415.9 35.9 reduce-scatter.7

commit v4 on v3

--- a/solution.py
+++ b/solution.py
@@ -172,37 +172,35 @@
         "htj,rhj->tr", grad_blocks, right_blocks, preferred_element_type=jnp.float32
     )
     back_low = butterfly_sum(back_part, "tensor").astype(jnp.bfloat16)
-    grad_up = lax.psum_scatter(up_parts, "dp", scatter_dimension=0, tiled=False).astype(jnp.float32)
-    row_part, low_row_part, grad_up, incoming = lax.optimization_barrier(
-        (back_low, low_sum, grad_up, incoming)
-    )
+    up_summed = lax.psum_scatter(up_parts, "dp", scatter_dimension=0, tiled=False)
+    left_parts = jnp.stack(
+        split_rows(
+            lax.dot_general(
+                back_low, inputs, (((0,), (0,)), ((), ())), preferred_element_type=jnp.float32
+            ),
+            0,
+            dp_size,
+        )
+    )
+    right_parts = jnp.stack(
+        split_rows(
+            jnp.einsum(
+                "tr,htj->rhj", low_sum, grad_blocks, preferred_element_type=jnp.float32
+            ).reshape(low_sum.shape[1], -1),
+            0,
+            dp_size,
+        )
+    )
+    joined = (jnp.concatenate([left_parts, right_parts], axis=2) * inv_root).astype(jnp.bfloat16)
+    joined, up_summed, incoming = lax.optimization_barrier((joined, up_summed, incoming))
+    joined = lax.psum_scatter(joined, "dp", scatter_dimension=0, tiled=False).astype(jnp.float32)
+    grad_up = jnp.transpose(up_summed.astype(jnp.float32), (2, 0, 1, 3))
     own_term = section_term(0)
     for level_bit in range(section_count - 1):
         own_term = own_term + incoming[level_bit].astype(jnp.float32)
     grad_input = (
         own_term + jnp.dot(back_low, low_left, preferred_element_type=jnp.float32)
     ).astype(jnp.bfloat16)
-    grad_up = jnp.transpose(grad_up, (2, 0, 1, 3))
-    left_parts = jnp.stack(
-        split_rows(
-            lax.dot_general(
-                row_part, inputs, (((0,), (0,)), ((), ())), preferred_element_type=jnp.float32
-            ),
-            0,
-            dp_size,
-        )
-    )
-    right_parts = jnp.stack(
-        split_rows(
-            jnp.einsum(
-                "tr,htj->rhj", low_row_part, grad_blocks, preferred_element_type=jnp.float32
-            ).reshape(low_row_part.shape[1], -1),
-            0,
-            dp_size,
-        )
-    )
-    joined = (jnp.concatenate([left_parts, right_parts], axis=2) * inv_root).astype(jnp.bfloat16)
-    joined = lax.psum_scatter(joined, "dp", scatter_dimension=0, tiled=False).astype(jnp.float32)
     grad_left = joined[:, :width_here]
     grad_right = joined[:, width_here:]
     return (grad_input, grad_up, grad_down, grad_left, grad_right)

time: 465 us -> 444 us (0.955)
  waiting for transfers between devices: 251 us -> 233 us
    reduce_scatter x1, waiting for transfers between devices: 58.7 us -> 41 us  [shards(): lax.psum_scatter(up_parts, 'dp', scatter_dimension=0, tiled=False)]
    unnamed x63 -> x65, local copies, waits for them, and re-layouts: 14.4 us -> 14.6 us
  transfers between devices with their start and end apart: 15 -> 15, of which waited for: 9 -> 9; matrix products, arithmetic and copies ran while one was open for 34% -> 40% of each run, Pallas kernels for 0% -> 0%
where the time goes in v4:
time: 444 us; the launch traced here: 440 us
  waiting for transfers between devices  233 us (52%)
  local copies, waits for them, and re-layouts  76 us (17%)
  matrix products  57 us (13%)
  other arithmetic  49 us (11%)
  between operations  14.6 us (3%)
  starting transfers between devices  10.9 us (2%)
    ppermute x2, waiting for transfers between devices, swap_shares(): got = lax.ppermute(send, 'groups', [(0, 1), (1, 0)])  58.9 us
    all_gather x2, waiting for transfers between devices, fetch_share(): return lax.all_gather(mine, 'dp', axis=0, tiled=False)  57.9 us
    reduce_scatter x1, waiting for transfers between devices, shards(): lax.psum_scatter(up_parts, 'dp', scatter_dimension=0, tiled=False)  41 us
    reduce_scatter x1, waiting for transfers between devices, shards(): lax.psum_scatter(down_parts, 'dp', scatter_dimension=0, tiled=False)  30.5 us
    ppermute x8, waiting for transfers between devices, swapped(): return lax.ppermute(block, axis, route)  26.3 us
    reduce_scatter x1, waiting for transfers between devices, shards(): lax.psum_scatter(joined, 'dp', scatter_dimension=0, tiled=False)  18 us
    another operation x5, other arithmetic, pick_blocks(): return jnp.stack(picked, axis=2)  15.9 us
    unnamed x65, local copies, waits for them, and re-layouts  14.6 us
  transfers between devices with their start and end apart: 15, of which 9 were waited for; matrix products, arithmetic and copies ran while one was open for 40% of the time, Pallas kernels for 0%

profile of v4, /device:TPU:0, one launch (start us, length us, event | category | flops | bytes accessed | tf_op | source)
XLA Modules:
  0.0 440.2 jit_solution(8173530824034915517)
XLA Ops:
  7.2 2.7 dynamic-slice_bitcast_fusion.1
  11.4 3.0 collective-permute-start.2
  18.4 57.9 %all-gather.5.cloned.1.call-done = bf16[128,16,3,256]{3,1,2,0:T(8,128)(2,1)} async-done(((bf16[32,16,3,256]{3,1,2,0:T(8,128)(2,1)}), bf16[128,16,3,256]{3,1,2,0:T(8,128)(2,1)}) %all-gather.5.cloned.1.call-update) | async-done | bytes 3145744 | tf_op jit(solution)/shard_map/all_gather | solution.py:29
  76.3 4.0 fusion.34
  94.4 4.8 %select_bitcast_fusion.3 = (bf16[256,16,1,256]{3,0,2,1:T(8,128)(2,1)}, bf16[256,16,1,256]{3,0,2,1:T(8,128)(2,1)}) fusion(bf16[16,256,256]{2,1,0:T(8,128)(2,1)} %gather_fusion.2, pred[16]{0:T(512)(128)(4,1)S(1)} %copy-done.26, bf16[16,256,256]{2,1,0:T(8,128)(2,1)} %gather_fusion.1, pred[16]{0:T(512)(128)(4,1)S(1)} %copy-done.27), kind=kLoop, calls=%fused_computation.87 | loop fusion | flops 2097152 | bytes 8388640 | tf_op jit(solution)/shard_map/stack | solution.py:97
  105.6 3.5 collective-permute-done.4
  116.1 4.8 %select_bitcast_fusion = (bf16[256,16,1,256]{3,0,2,1:T(8,128)(2,1)}, bf16[256,16,1,256]{3,0,2,1:T(8,128)(2,1)}) fusion(bf16[16,256,256]{2,1,0:T(8,128)(2,1)} %gather_fusion.5, pred[16]{0:T(512)(128)(4,1)S(1)} %get-tuple-element.76, bf16[16,256,256]{2,1,0:T(8,128)(2,1)} %gather_fusion.4, pred[16]{0:T(512)(128)(4,1)S(1)} %get-tuple-element.78), kind=kLoop, calls=%fused_computation.84 | loop fusion | flops 2097152 | bytes 8388640 | tf_op jit(solution)/shard_map/stack | solution.py:97
  120.9 12.6 %collective-permute-done = bf16[3,32,16,3,256]{4,2,3,1,0:T(8,128)(2,1)} collective-permute-done((bf16[3,32,16,3,256]{4,2,3,1,0:T(8,128)(2,1)}, bf16[3,32,16,3,256]{4,2,3,1,0:T(8,128)(2,1)}, u32[]{:S(2)}, u32[]{:S(2)}) %collective-permute-start) | collective-permute-done | bytes 2359328 | tf_op jit(solution)/shard_map/ppermute | solution.py:47
  133.5 3.5 fusion.23
  137.0 4.4 fusion.7
  141.4 11.1 %fusion.8 = f32[16,256,256,1]{1,2,3,0:T(8,128)} fusion(bf16[256,16,3,256]{3,1,2,0:T(8,128)(2,1)S(1)} %bitcast.214, bf16[256,16,1,256]{3,0,2,1:T(8,128)(2,1)} %get-tuple-element.82, bf16[256,16,1,256]{3,0,2,1:T(8,128)(2,1)} %get-tuple-element.83, bf16[256,16,1,256]{3,0,2,1:T(8,128)(2,1)} %select_bitcast_fusion.2), kind=kOutput, calls=%fused_computation.38 | convolution fusion | flops 1616904192 | bytes 16777216 | tf_op jit(solution)/shard_map/thsi,ihsj->htj/dot_general | solution.py:117
  152.5 6.4 %multiply_convert_fusion = (bf16[16,256,256]{1,2,0:T(8,128)(2,1)S(1)}, f32[16,256,256]{1,2,0:T(8,128)}) fusion(bf16[256,128,1]{1,0,2:T(8,128)(2,1)S(1)} %fusion.63, bf16[16,16,8,256]{3,2,1,0:T(8,128)(2,1)} %bitcast.230, f32[16,256,256,1]{1,2,3,0:T(8,128)} %fusion.8), kind=kOutput, calls=%fused_computation.50 | convolution fusion | flops 278921216 | bytes 11599872 | tf_op jit(solution)/shard_map/tr,rhj->htj/dot_general | solution.py:123
  165.3 4.2 fusion
  169.6 2.7 fusion.33
  173.8 3.1 pad_maximum_fusion.1
  178.0 46.3 %collective-permute-done.5 = bf16[3,32,16,3,256]{4,2,3,1,0:T(8,128)(2,1)S(1)} collective-permute-done((bf16[3,32,16,3,256]{4,2,3,1,0:T(8,128)(2,1)S(1)}, bf16[3,32,16,3,256]{4,2,3,1,0:T(8,128)(2,1)S(1)}, u32[]{:S(2)}, u32[]{:S(2)}) %collective-permute-start.5) | collective-permute-done | bytes 2359328 | tf_op jit(solution)/shard_map/ppermute | solution.py:47
  227.5 3.6 fusion.4
  231.1 6.3 %fusion.16 = bf16[16,256,256]{1,2,0:T(8,128)(2,1)S(1)} fusion(f32[16,256,256]{1,2,0:T(8,128)} %get-tuple-element.81, bf16[256,16,3,256]{3,0,2,1:T(8,128)(2,1)S(1)} %bitcast.224, bf16[256,16,1,256]{3,0,2,1:T(8,128)(2,1)S(1)} %copy-done.14, bf16[256,16,1,256]{3,0,2,1:T(8,128)(2,1)S(1)} %copy-done.16, bf16[256,16,1,256]{3,0,2,1:T(8,128)(2,1)S(1)} %copy-done.21), kind=kOutput, calls=%fused_computation.48 | convolution fusion | flops 1636827136 | bytes 18874368 | tf_op jit(solution)/shard_map/thso,jhso->htj/dot_general | solution.py:141
  241.1 2.6 fusion.44
  244.7 4.0 fusion.1
  248.8 30.5 %reduce-scatter.4.cloned.1.call-done = bf16[1,16,64,3,256]{4,2,3,1,0:T(8,128)(2,1)} async-done(((bf16[4,16,64,3,256]{4,2,3,1,0:T(8,128)(2,1)}), bf16[1,16,64,3,256]{4,2,3,1,0:T(8,128)(2,1)}) %reduce-scatter.4.cloned.1.call-update) | async-done | bytes 1572880 | tf_op jit(solution)/shard_map/reduce_scatter | solution.py:140
  279.4 5.7 %fusion.74 = (bf16[256,16,1,256]{3,1,2,0:T(8,128)(2,1)}, bf16[256,16,1,256]{3,1,2,0:T(8,128)(2,1)}, bf16[256,16,1,256]{3,1,2,0:T(8,128)(2,1)}) fusion(bf16[256,16,3,256]{3,1,2,0:T(8,128)(2,1)} %bitcast.215), kind=kLoop, calls=%fused_computation.153 | loop fusion | bytes 12582912 | tf_op jit(solution)/shard_map/slice | solution.py:157
  306.3 4.7 %copy.135 = bf16[256,16,256]{2,1,0:T(8,128)(2,1)} copy(bf16[256,16,256]{0,2,1:T(8,128)(2,1)} %convolution_bitcast_fusion.1) | data formatting | bytes 4194304 | tf_op jit(solution)/shard_map/htj,ihj->thi/transpose | solution.py:154
  317.1 4.6 %copy.138 = bf16[256,16,256]{2,1,0:T(8,128)(2,1)} copy(bf16[256,16,256]{0,2,1:T(8,128)(2,1)} %convolution_bitcast_fusion) | data formatting | bytes 4194304 | tf_op jit(solution)/shard_map/htj,ihj->thi/transpose | solution.py:154
  329.0 22.7 %collective-permute-done.9 = bf16[256,2048]{1,0:T(8,128)(2,1)} collective-permute-done((bf16[256,2048]{1,0:T(8,128)(2,1)}, bf16[256,2048]{1,0:T(8,128)(2,1)}, u32[]{:S(2)}, u32[]{:S(2)}) %collective-permute-start.9) | collective-permute-done | bytes 1048608 | tf_op jit(solution)/shard_map/ppermute | solution.py:19
  351.8 41.0 %reduce-scatter.6.cloned.1.call-done = bf16[1,16,3,64,256]{4,3,2,1,0:T(8,128)(2,1)} async-done(((bf16[4,16,3,64,256]{4,3,2,1,0:T(8,128)(2,1)}), bf16[1,16,3,64,256]{4,3,2,1,0:T(8,128)(2,1)}) %reduce-scatter.6.cloned.1.call-update) | async-done | bytes 1572880 | tf_op jit(solution)/shard_map/reduce_scatter | solution.py:175
  392.8 3.8 convolution_bitcast_fusion.2
  396.6 3.3 copy.116
  402.4 3.5 copy.140
  406.3 3.5 copy.139
  409.8 3.1 add_convert_fusion
  412.9 18.0 %reduce-scatter.8.cloned.1.call-done = bf16[1,32,6144]{2,1,0:T(8,128)(2,1)} async-done(((bf16[4,32,6144]{2,1,0:T(8,128)(2,1)}), bf16[1,32,6144]{2,1,0:T(8,128)(2,1)}) %reduce-scatter.8.cloned.1.call-update) | async-done | bytes 393232 | tf_op jit(solution)/shard_map/reduce_scatter | solution.py:196
  (150 shorter events, 89.6 us)
Async XLA Ops:
  7.2 7.2 %copy-start = (bf16[128,2048]{1,0:T(8,128)(2,1)S(1)}, bf16[128,2048]{1,0:T(8,128)(2,1)}, u32[]{:S(2)}) copy-start(bf16[128,2048]{1,0:T(8,128)(2,1)} %param.14) | copy-start | bytes 1572868
  7.2 69.1 %all-gather.5.cloned.1.call-start = ((), (), s32[]{:S(2)}) async-start(), calls=%async_computation.6 | async-start | bytes 3932160 | tf_op jit(solution)/shard_map/all_gather | solution.py:29
  10.0 159.5 %all-gather.7.cloned.1.call-start = ((), (), s32[]{:S(2)}) async-start(), calls=%async_computation.7 | async-start | bytes 3932160 | tf_op jit(solution)/shard_map/all_gather | solution.py:29
  11.4 6.5 %copy-start.28 = (s32[16,3]{0,1:T(4,128)S(1)}, s32[16,3]{0,1:T(4,128)}, u32[]{:S(2)}) copy-start(s32[16,3]{0,1:T(4,128)} %param.17) | copy-start | bytes 580
  11.4 97.8 %collective-permute-start.2 = (bf16[256,2048]{0,1:T(8,128)(2,1)}, bf16[256,2048]{0,1:T(8,128)(2,1)}, u32[]{:S(2)}, u32[]{:S(2)}) collective-permute-start(bf16[256,2048]{0,1:T(8,128)(2,1)} %copy.104), channel_id=1, source_target_pairs={{0,2},{2,0},{1,3},{3,1},{4,6},{6,4},{5,7},{7,5},{8,10},{10,8},{9,1... | collective-permute-start | bytes 3145736 | tf_op jit(solution)/shard_map/ppermute | solution.py:19
  14.3 96.3 %collective-permute-start.1 = (bf16[256,2048]{0,1:T(8,128)(2,1)}, bf16[256,2048]{0,1:T(8,128)(2,1)}, u32[]{:S(2)}, u32[]{:S(2)}) collective-permute-start(bf16[256,2048]{0,1:T(8,128)(2,1)} %copy.104), channel_id=1, source_target_pairs={{0,1},{1,0},{2,3},{3,2},{4,5},{5,4},{6,7},{7,6},{8,9},{9,8},{10,11... | collective-permute-start | bytes 3145736 | tf_op jit(solution)/shard_map/ppermute | solution.py:19
  14.8 88.4 %collective-permute-start.3 = (f32[256,128]{1,0:T(8,128)S(1)}, f32[256,128]{1,0:T(8,128)}, u32[]{:S(2)}, u32[]{:S(2)}) collective-permute-start(f32[256,128]{1,0:T(8,128)S(1)} %fusion.76), channel_id=1, source_target_pairs={{0,1},{1,0},{2,3},{3,2},{4,5},{5,4},{6,7},{7,6},{8,9},{9,8},{10,11... | collective-permute-start | bytes 393224 | tf_op jit(solution)/shard_map/ppermute | solution.py:19
  17.8 261.5 %reduce-scatter.4.cloned.1.call-start = ((), (), s32[]{:S(2)}) async-start(), calls=%async_computation.3 | async-start | bytes 7864320 | tf_op jit(solution)/shard_map/reduce_scatter | solution.py:140
  76.3 7.2 %copy-start.24 = (bf16[256,2048]{1,0:T(8,128)(2,1)S(1)}, bf16[256,2048]{1,0:T(8,128)(2,1)}, u32[]{:S(2)}) copy-start(bf16[256,2048]{1,0:T(8,128)(2,1)} %param.11) | copy-start | bytes 3145732
  80.3 53.1 %collective-permute-start = (bf16[3,32,16,3,256]{4,2,3,1,0:T(8,128)(2,1)}, bf16[3,32,16,3,256]{4,2,3,1,0:T(8,128)(2,1)}, u32[]{:S(2)}, u32[]{:S(2)}) collective-permute-start(bf16[3,32,16,3,256]{4,2,3,1,0:T(8,128)(2,1)} %fusion.34), channel_id=1, source_target_pairs={{0,16},{16,0},{1,17},{17,1},{2,18},{18,2},{3,19},{19,3},{4,20},{20... | collective-permute-start | bytes 7077896 | tf_op jit(solution)/shard_map/ppermute | solution.py:47
  94.4 4.8 %copy-start.11 = (bf16[16,256,256]{2,1,0:T(8,128)(2,1)S(1)}, bf16[16,256,256]{2,1,0:T(8,128)(2,1)}, u32[]{:S(2)}) copy-start(bf16[16,256,256]{2,1,0:T(8,128)(2,1)} %gather_fusion.3) | copy-start | bytes 6291460
  104.1 5.0 %collective-permute-start.4 = (f32[256,128]{1,0:T(8,128)S(1)}, f32[256,128]{1,0:T(8,128)S(1)}, u32[]{:S(2)}, u32[]{:S(2)}) collective-permute-start(f32[256,128]{1,0:T(8,128)S(1)} %add.88), channel_id=1, source_target_pairs={{0,2},{2,0},{1,3},{3,1},{4,6},{6,4},{5,7},{7,5},{8,10},{10,8},{9,1... | collective-permute-start | bytes 393224 | tf_op jit(solution)/shard_map/ppermute | solution.py:19
  116.1 17.4 %copy-start.12 = (bf16[1,32,16,3,256]{4,2,3,1,0:T(8,128)(2,1)S(1)}, bf16[1,32,16,3,256]{4,2,3,1,0:T(8,128)(2,1)}, u32[]{:S(2)}) copy-start(bf16[1,32,16,3,256]{4,2,3,1,0:T(8,128)(2,1)} %get-tuple-element.63) | copy-start | bytes 2359300
  141.4 11.1 %copy-start.1 = (bf16[4,2,32,16,3,256]{5,3,4,2,1,0:T(8,128)(2,1)}, bf16[4,2,32,16,3,256]{5,3,4,2,1,0:T(8,128)(2,1)S(1)}, u32[]{:S(2)}) copy-start(bf16[4,2,32,16,3,256]{5,3,4,2,1,0:T(8,128)(2,1)S(1)} %fusion.7) | copy-start | bytes 18874372
  152.5 6.4 %copy-start.13 = (bf16[256,16,1,256]{3,0,2,1:T(8,128)(2,1)S(1)}, bf16[256,16,1,256]{3,0,2,1:T(8,128)(2,1)}, u32[]{:S(2)}) copy-start(bf16[256,16,1,256]{3,0,2,1:T(8,128)(2,1)} %get-tuple-element.84) | copy-start | bytes 6291460
  152.5 6.4 %copy-start.15 = (bf16[256,16,1,256]{3,0,2,1:T(8,128)(2,1)S(1)}, bf16[256,16,1,256]{3,0,2,1:T(8,128)(2,1)}, u32[]{:S(2)}) copy-start(bf16[256,16,1,256]{3,0,2,1:T(8,128)(2,1)} %get-tuple-element.85) | copy-start | bytes 6291460
  152.5 6.4 %copy-start.20 = (bf16[256,16,1,256]{3,0,2,1:T(8,128)(2,1)S(1)}, bf16[256,16,1,256]{3,0,2,1:T(8,128)(2,1)}, u32[]{:S(2)}) copy-start(bf16[256,16,1,256]{3,0,2,1:T(8,128)(2,1)} %select_bitcast_fusion.5) | copy-start | bytes 6291460
  169.5 4.3 copy-start.6
  169.5 223.3 %reduce-scatter.6.cloned.1.call-start = ((), (), s32[]{:S(2)}) async-start(), calls=%async_computation.4 | async-start | bytes 7864320 | tf_op jit(solution)/shard_map/reduce_scatter | solution.py:175
  169.6 4.2 copy-start.7
  172.3 4.7 %copy-start.2 = (bf16[128,16,3,256]{3,1,2,0:T(8,128)(2,1)S(1)}, bf16[128,16,3,256]{3,1,2,0:T(8,128)(2,1)}, u32[]{:S(2)}) copy-start(bf16[128,16,3,256]{3,1,2,0:T(8,128)(2,1)} %all-gather.7.cloned.1.call-done) | copy-start | bytes 9437188
  172.3 52.0 %collective-permute-start.5 = (bf16[3,32,16,3,256]{4,2,3,1,0:T(8,128)(2,1)S(1)}, bf16[3,32,16,3,256]{4,2,3,1,0:T(8,128)(2,1)S(1)}, u32[]{:S(2)}, u32[]{:S(2)}) collective-permute-start(bf16[3,32,16,3,256]{4,2,3,1,0:T(8,128)(2,1)S(1)} %fusion.33), channel_id=1, source_target_pairs={{0,16},{16,0},{1,17},{17,1},{2,18},{18,2},{3,19},{19,3},{4,20},{20... | collective-permute-start | bytes 7077896 | tf_op jit(solution)/shard_map/ppermute | solution.py:47
  227.4 3.7 copy-start.14
  227.4 3.7 copy-start.16
  227.4 3.7 copy-start.21
  279.3 151.6 %reduce-scatter.8.cloned.1.call-start = ((), (), s32[]{:S(2)}) async-start(), calls=%async_computation.5 | async-start | bytes 1966080 | tf_op jit(solution)/shard_map/reduce_scatter | solution.py:196
  304.0 17.7 %collective-permute-start.6 = (f32[256,128]{1,0:T(8,128)S(1)}, f32[256,128]{1,0:T(8,128)S(1)}, u32[]{:S(2)}, u32[]{:S(2)}) collective-permute-start(f32[256,128]{1,0:T(8,128)S(1)} %convolution_bitcast_fusion.7), channel_id=1, source_target_pairs={{0,1},{1,0},{2,3},{3,2},{4,5},{5,4},{6,7},{7,6},{8,9},{9,8},{10,11... | collective-permute-start | bytes 393224 | tf_op jit(solution)/shard_map/ppermute | solution.py:19
  311.0 3.9 copy-start.8
  314.4 14.6 %collective-permute-start.8 = (bf16[256,2048]{1,0:T(8,128)(2,1)}, bf16[256,2048]{1,0:T(8,128)(2,1)}, u32[]{:S(2)}, u32[]{:S(2)}) collective-permute-start(bf16[256,2048]{1,0:T(8,128)(2,1)} %bitcast.98), channel_id=1, source_target_pairs={{0,1},{1,0},{2,3},{3,2},{4,5},{5,4},{6,7},{7,6},{8,9},{9,8},{10,11... | collective-permute-start | bytes 3145736 | tf_op jit(solution)/shard_map/ppermute | solution.py:19
  321.7 5.5 %copy-start.5 = (bf16[256,2048]{1,0:T(8,128)(2,1)S(1)}, bf16[256,2048]{1,0:T(8,128)(2,1)}, u32[]{:S(2)}) copy-start(bf16[256,2048]{1,0:T(8,128)(2,1)} %param.10) | copy-start | bytes 3145732
  321.7 5.5 %collective-permute-start.7 = (f32[256,128]{1,0:T(8,128)S(1)}, f32[256,128]{1,0:T(8,128)S(1)}, u32[]{:S(2)}, u32[]{:S(2)}) collective-permute-start(f32[256,128]{1,0:T(8,128)S(1)} %add.95), channel_id=1, source_target_pairs={{0,2},{2,0},{1,3},{3,1},{4,6},{6,4},{5,7},{7,5},{8,10},{10,8},{9,1... | collective-permute-start | bytes 393224 | tf_op jit(solution)/shard_map/ppermute | solution.py:19
  326.6 25.1 %collective-permute-start.9 = (bf16[256,2048]{1,0:T(8,128)(2,1)}, bf16[256,2048]{1,0:T(8,128)(2,1)}, u32[]{:S(2)}, u32[]{:S(2)}) collective-permute-start(bf16[256,2048]{1,0:T(8,128)(2,1)} %bitcast.100), channel_id=1, source_target_pairs={{0,2},{2,0},{1,3},{3,1},{4,6},{6,4},{5,7},{7,5},{8,10},{10,8},{9,1... | collective-permute-start | bytes 3145736 | tf_op jit(solution)/shard_map/ppermute | solution.py:19
  (12 other events, 29.1 us)
Sparse Core Ops, SparseCore 0:
  10.1 66.1 all-gather.4
  77.9 62.0 all-gather.6
  169.6 109.6 reduce-scatter.3
  281.4 111.2 reduce-scatter.5
  394.9 35.9 reduce-scatter.7
